TPU v7x, 512 devices: a whole 4x4x16 slice. The times are simulated.
512 devices in a mesh: ctx: 64 (over z, x), ch: 8 (over y, core).
Axes of the slice: x: 4, y: 4, z: 16, core: 2. Of those that a mesh axis runs over, the one named last changes fastest.
Arguments:
- query: bfloat16 [8192, 4096], P('ctx', 'ch'), may hold values from -6 to 6
- key: bfloat16 [8192, 4096], P('ctx', 'ch'), may hold values from -6 to 6
- value: bfloat16 [8192, 4096], P('ctx', 'ch'), may hold values from -6 to 6
- filter_taps: float32 [8192, 256], P('ctx', 'ch'), may hold values from -0.0625 to 0.0625
- conv_bias: float32 [4096], P('ch'), may hold values from -4 to 4
- norm_gain: float32 [4096], P('ch'), may hold values from 0.1 to 1.9
- pair_list: int32 [2080, 3], replicated, may hold values from 0 to 63, as said below
Outputs:
- mixed: bfloat16 [8192, 4096], P('ctx', 'ch')
Inputs may be any that keep to these rules, and one draw needn't show every extreme that they name: `pair_list`: every pair of blocks with source <= target appears once, in no particular order. A row with source = target names the device that holds that block; blocks c and 63 - c are held by two devices whose indices differ only in the lowest bit. Every other pair is executed by one of those two devices for its target block. Each device executes at most 33 pairs.
All inputs are finite; a program needn't handle non-finite values.
Results may differ from a plain program's by a relative error of at most 0.0049.
Values may be sent and summed in bfloat16 or wider, within the bound.
No kernel may reach another device: no remote copies, remote signals or barrier semaphores. Data moves between devices by JAX's collectives and lax.ppermute only.
A program may use at most 64 MiB of HBM per device.

v0:
```python
import jax
import jax.numpy as jnp
from jax import lax
from jax.experimental import pallas as pl
from jax.experimental.pallas import tpu as pltpu
from jax.sharding import PartitionSpec as P


def placement(pair_list, blocks):
    source = pair_list[:, 0]
    target = pair_list[:, 1]
    runner = pair_list[:, 2]
    slots = lax.iota(jnp.int32, blocks)
    on_diag = source == target
    holds = on_diag[:, None] & (runner[:, None] == slots[None, :])
    holder = jnp.sum(jnp.where(holds, source[:, None], 0), axis=0)
    keeps = on_diag[:, None] & (source[:, None] == slots[None, :])
    device_of = jnp.sum(jnp.where(keeps, runner[:, None], 0), axis=0)
    return holder, device_of


def to_bf16_grid(values):
    return lax.reduce_precision(values, exponent_bits=8, mantissa_bits=7)


def conv_kernel(width, window_ref, signal_ref, out_ref):
    rows = out_ref.shape[0]
    lanes = out_ref.shape[1]
    blocks = window_ref.shape[0]
    signal = signal_ref[...].astype(jnp.float32)
    lane = lax.broadcasted_iota(jnp.int32, (rows, lanes), 1)

    def step(lag, total):
        window = jnp.broadcast_to(window_ref[pl.ds(lag, 1), :], (rows, 2 * rows))
        skewed = pltpu.roll(window, rows + 1, 1, stride=1, stride_axis=0)
        block = skewed[:, :rows]
        block_hi = block.astype(jnp.bfloat16)
        block_lo = (block - block_hi.astype(jnp.float32)).astype(jnp.bfloat16)
        moved = pltpu.roll(signal, lag * width, 1)
        moved = jnp.where(lane >= lag * width, moved, 0.0).astype(jnp.bfloat16)
        total = total + jnp.dot(block_hi, moved, preferred_element_type=jnp.float32)
        total = total + jnp.dot(block_lo, moved, preferred_element_type=jnp.float32)
        return total

    out_ref[...] = lax.fori_loop(
        0, blocks, step, jnp.zeros((rows, lanes), jnp.float32), unroll=2
    )


def causal_conv(window, signal, width):
    rows, lanes = signal.shape
    blocks = window.shape[0]
    return pl.pallas_call(
        lambda *refs: conv_kernel(width, *refs),
        out_shape=jax.ShapeDtypeStruct((rows, lanes), jnp.float32),
        in_specs=[pl.BlockSpec(memory_space=pltpu.VMEM)] * 2,
        out_specs=pl.BlockSpec(memory_space=pltpu.VMEM),
        cost_estimate=pl.CostEstimate(
            flops=4 * rows * rows * lanes * blocks,
            bytes_accessed=window.size * 4 + signal.size * 2 + rows * lanes * 4,
            transcendentals=0,
        ),
    )(window, signal)


def body(query, key, value, filter_taps, conv_bias, norm_gain, pair_list):
    rows = query.shape[0]
    channels = query.shape[1]
    groups = filter_taps.shape[1]
    blocks = lax.axis_size("ctx")
    width = channels // blocks
    share = (channels // groups) // width
    holder, device_of = placement(pair_list, blocks)

    product = to_bf16_grid(key.astype(jnp.float32) * value.astype(jnp.float32))
    signal = product.astype(jnp.bfloat16)

    taps_hi = to_bf16_grid(filter_taps)
    taps_lo = filter_taps - taps_hi
    coded = jnp.stack([taps_hi.T, taps_lo.T], axis=1).reshape(groups, 2, rows // width, width)
    coded = jnp.repeat(coded, share, axis=0).reshape(blocks, 2 * rows // width, width)
    coded = coded.transpose(1, 0, 2).reshape(2 * rows // width, channels)
    outgoing = jnp.concatenate([signal, coded.astype(jnp.bfloat16)], axis=0)

    incoming = lax.all_to_all(outgoing, "ctx", 1, 0, tiled=True)
    incoming = incoming.reshape(blocks, rows + 2 * rows // width, width)
    in_order = incoming[:, :rows, :][device_of]
    taps_in = incoming[:, rows:, :].astype(jnp.float32).reshape(blocks, 2, rows)
    my_taps = taps_in[:, 0, :] + taps_in[:, 1, :]
    earlier = jnp.concatenate([jnp.zeros((1, rows), jnp.float32), my_taps[:-1]], axis=0)
    window = jnp.concatenate([earlier, my_taps], axis=1)[:, ::-1]

    lined = in_order.transpose(1, 0, 2).reshape(rows, blocks * width)
    conv = causal_conv(window, lined, width)
    conv = conv.reshape(rows, blocks, width)[:, holder, :]
    conv = lax.all_to_all(conv, "ctx", 1, 1, tiled=True).reshape(rows, channels)

    long_conv = conv + conv_bias[None, :] * product
    gated = query.astype(jnp.float32) * long_conv
    squares = jnp.sum(gated * gated, axis=1)
    total_sq = lax.psum(squares, "ch")
    scaling = lax.rsqrt(total_sq / (channels * lax.axis_size("ch")) + 1e-05)
    return (gated * scaling[:, None] * norm_gain[None, :]).astype(jnp.bfloat16)


def solution(mesh):
    placed = (P("ctx", "ch"), P("ctx", "ch"), P("ctx", "ch"), P("ctx", "ch"), P("ch"), P("ch"), P())
    return jax.shard_map(
        body, mesh=mesh, in_specs=placed, out_specs=P("ctx", "ch"), check_vma=False
    )
```

profile of v0, /device:TPU:1, one launch (start us, length us, event | category | flops | bytes accessed | tf_op | source)
XLA Modules:
  0.0 105.8 jit_solution(1041778793808304858)
XLA Ops:
  0.0 1.1 copy.59
  1.1 0.0 copy-done
  1.1 0.1 copy.60
  1.2 0.0 copy-done.3
  1.2 0.1 copy.61
  1.3 0.1 copy.62
  1.5 0.2 copy.63
  1.7 0.1 broadcast_in_dim.31
  1.8 0.1 convert_element_type.31
  2.0 0.7 maximum_bitcast_fusion
  2.8 19.2 %all-to-all-start = ((bf16[160,64,8]{0,2,1:T(8,128)(2,1)}), bf16[160,64,8]{0,2,1:T(8,128)(2,1)S(1)}, u32[]{:S(2)}, u32[]{:S(2)}) async-start(bf16[160,64,8]{0,2,1:T(8,128)(2,1)} %maximum_bitcast_fusion), calls=%async_computation | async-start | bytes 524288 | tf_op jit(solution)/shard_map/all_to_all | solution.py:85
  22.1 0.3 select_reduce_fusion
  22.5 18.7 %all-to-all-done = bf16[160,64,8]{0,2,1:T(8,128)(2,1)S(1)} async-done(((bf16[160,64,8]{0,2,1:T(8,128)(2,1)}), bf16[160,64,8]{0,2,1:T(8,128)(2,1)S(1)}, u32[]{:S(2)}, u32[]{:S(2)}) %all-to-all-start) | async-done | bytes 163872 | tf_op jit(solution)/shard_map/all_to_all | solution.py:85
  41.2 0.3 copy.64
  41.6 0.1 copy.71
  41.7 0.1 copy.72
  41.8 0.8 rev.3.refs_0_
  42.6 0.2 copy.67
  42.8 0.6 gather_fusion
  43.5 0.8 copy.68.refs_1_
  44.2 14.9 %shard_map.73 = f32[128,512]{1,0:T(8,128)} custom-call(f32[64,256]{1,0:T(8,128)} %rev.3.refs_0_, bf16[128,512]{1,0:T(8,128)(2,1)} %copy.68.refs_1_), custom_call_target="tpu_custom_call" | custom-call | flops 2147483648 | bytes 458752 | tf_op jit(solution)/shard_map/pallas_call | solution.py:53
  59.1 1.1 %copy.69 = f32[128,512]{0,1:T(8,128)S(1)} copy(f32[128,512]{1,0:T(8,128)} %shard_map.73) | data formatting | bytes 524288 | tf_op jit(solution)/shard_map/pallas_call | solution.py:53
  60.2 1.3 %gather_fusion.1 = f32[64,128,8]{1,2,0:T(8,128)} fusion(f32[128,64,8]{0,2,1:T(8,128)S(1)} %bitcast.42, s32[1024]{0:T(1024)S(1)} %pad_clamp_fusion), kind=kCustom, calls=%fused_computation.1 | custom fusion | bytes 524544 | tf_op jit(solution)/shard_map/gather | solution.py:95
  61.5 7.5 %all-to-all-start.1 = ((f32[128,64,8]{0,2,1:T(8,128)}), f32[128,64,8]{0,2,1:T(8,128)S(1)}, u32[]{:S(2)}, u32[]{:S(2)}) async-start(f32[128,64,8]{0,2,1:T(8,128)} %bitcast.18), calls=%async_computation.1 | async-start | bytes 524288 | tf_op jit(solution)/shard_map/all_to_all | solution.py:96
  69.0 0.0 copy-done.1
  69.0 0.1 copy.58
  69.1 0.0 copy-start.5
  69.2 18.2 %all-to-all-done.1 = f32[128,64,8]{0,2,1:T(8,128)S(1)} async-done(((f32[128,64,8]{0,2,1:T(8,128)}), f32[128,64,8]{0,2,1:T(8,128)S(1)}, u32[]{:S(2)}, u32[]{:S(2)}) %all-to-all-start.1) | async-done | bytes 262176 | tf_op jit(solution)/shard_map/all_to_all | solution.py:96
  87.4 0.2 multiply_reduce_fusion
  87.5 17.2 %psum.7 = f32[128]{0:T(128)S(1)} all-reduce(f32[128]{0:T(128)S(1)} %multiply_reduce_fusion), channel_id=1, replica_groups=mesh['ctx'=64,'ch'=8] {'ch'}, use_global_device_ids=true, to_apply=%region_3.4 | all-reduce | flops 128 | bytes 1024 | tf_op jit(solution)/shard_map/psum | solution.py:101
  104.8 0.2 multiply_convert_fusion
  105.0 0.8 copy.70
  (24 shorter events, 0.3 us)
Async XLA Ops:
  0.0 1.1 %copy-start = (bf16[128,512]{1,0:T(8,128)(2,1)S(1)}, bf16[128,512]{1,0:T(8,128)(2,1)}, u32[]{:S(2)}) copy-start(bf16[128,512]{1,0:T(8,128)(2,1)} %param.9) | copy-start | bytes 393220
  0.0 1.2 %copy-start.3 = (f32[128,32]{0,1:T(8,128)S(1)}, f32[128,32]{0,1:T(8,128)}, u32[]{:S(2)}) copy-start(f32[128,32]{0,1:T(8,128)} %param.10) | copy-start | bytes 49156
  2.8 19.3 %copy-start.2 = (s32[2080,3]{0,1:T(4,128)S(1)}, s32[2080,3]{0,1:T(4,128)}, u32[]{:S(2)}) copy-start(s32[2080,3]{0,1:T(4,128)} %param.13) | copy-start | bytes 74884
  2.8 38.5 %all-to-all-start = ((bf16[160,64,8]{0,2,1:T(8,128)(2,1)}), bf16[160,64,8]{0,2,1:T(8,128)(2,1)S(1)}, u32[]{:S(2)}, u32[]{:S(2)}) async-start(bf16[160,64,8]{0,2,1:T(8,128)(2,1)} %maximum_bitcast_fusion), calls=%async_computation | async-start | bytes 524288 | tf_op jit(solution)/shard_map/all_to_all | solution.py:85
  61.5 7.5 %copy-start.1 = (bf16[128,512]{1,0:T(8,128)(2,1)S(1)}, bf16[128,512]{1,0:T(8,128)(2,1)}, u32[]{:S(2)}) copy-start(bf16[128,512]{1,0:T(8,128)(2,1)} %param.7) | copy-start | bytes 393220
  61.5 25.9 %copy-start.4 = (f32[512]{0:T(512)S(1)}, f32[512]{0:T(512)}, u32[]{:S(2)}) copy-start(f32[512]{0:T(512)} %param.11) | copy-start | bytes 6148
  61.5 25.9 %all-to-all-start.1 = ((f32[128,64,8]{0,2,1:T(8,128)}), f32[128,64,8]{0,2,1:T(8,128)S(1)}, u32[]{:S(2)}, u32[]{:S(2)}) async-start(f32[128,64,8]{0,2,1:T(8,128)} %bitcast.18), calls=%async_computation.1 | async-start | bytes 524288 | tf_op jit(solution)/shard_map/all_to_all | solution.py:96
  69.1 35.6 %copy-start.5 = (f32[512]{0:T(512)S(1)}, f32[512]{0:T(512)}, u32[]{:S(2)}) copy-start(f32[512]{0:T(512)} %param.12) | copy-start | bytes 6148
where the time goes:
time: 106 us
  waiting for transfers between devices  36.9 us (35%)
  starting transfers between devices  26.7 us (25%)
  blocking collectives  17.2 us (16%)
  Pallas kernels  14.9 us (14%)
  local copies, waits for them, and re-layouts  8.12 us (8%)
  other arithmetic  1.62 us (2%)
    all_to_all x1, starting transfers between devices, body(): incoming = lax.all_to_all(outgoing, 'ctx', 1, 0, tiled=True)  19.2 us
    all_to_all x1, waiting for transfers between devices, body(): incoming = lax.all_to_all(outgoing, 'ctx', 1, 0, tiled=True)  18.7 us
    all_to_all x1, waiting for transfers between devices, body(): conv = lax.all_to_all(conv, 'ctx', 1, 1, tiled=True).reshape(rows, channels)  18.2 us
    psum x1, blocking collectives, body(): total_sq = lax.psum(squares, 'ch')  17.2 us
    pallas_call x1, Pallas kernels, causal_conv(): pl.pallas_call(lambda *refs: conv_kernel(width, *refs), out_shape=jax.Sha...  14.9 us
    all_to_all x1, starting transfers between devices, body(): conv = lax.all_to_all(conv, 'ctx', 1, 1, tiled=True).reshape(rows, channels)  7.49 us
  transfers between devices with their start and end apart: 2, of which 2 were waited for; matrix products, arithmetic and copies ran while one was open for 1% of the time, Pallas kernels for 0%

commit v1 on v0

--- a/solution.py
+++ b/solution.py
@@ -38,9 +38,9 @@
         block_lo = (block - block_hi.astype(jnp.float32)).astype(jnp.bfloat16)
         moved = pltpu.roll(signal, lag * width, 1)
         moved = jnp.where(lane >= lag * width, moved, 0.0).astype(jnp.bfloat16)
-        total = total + jnp.dot(block_hi, moved, preferred_element_type=jnp.float32)
-        total = total + jnp.dot(block_lo, moved, preferred_element_type=jnp.float32)
-        return total
+        pair = jnp.concatenate([block_hi, block_lo], axis=1)
+        both = jnp.concatenate([moved, moved], axis=0)
+        return total + jnp.dot(pair, both, preferred_element_type=jnp.float32)
 
     out_ref[...] = lax.fori_loop(
         0, blocks, step, jnp.zeros((rows, lanes), jnp.float32), unroll=2
@@ -98,7 +98,7 @@
     long_conv = conv + conv_bias[None, :] * product
     gated = query.astype(jnp.float32) * long_conv
     squares = jnp.sum(gated * gated, axis=1)
-    total_sq = lax.psum(squares, "ch")
+    total_sq = jnp.sum(lax.all_gather(squares, "ch"), axis=0)
     scaling = lax.rsqrt(total_sq / (channels * lax.axis_size("ch")) + 1e-05)
     return (gated * scaling[:, None] * norm_gain[None, :]).astype(jnp.bfloat16)
 

time: 106 us -> 104 us (0.981)
  blocking collectives: 17.2 us -> 15.8 us
  Pallas kernels: 14.9 us -> 13.8 us
    psum x1 -> x0, blocking collectives: 17.2 us -> none  [body(): total_sq = lax.psum(squares, 'ch')]
    all_gather x0 -> x1, blocking collectives: none -> 15.8 us  [body(): total_sq = jnp.sum(lax.all_gather(squares, 'ch'), axis=0)]
where the time goes in v1:
time: 104 us; the launch traced here: 103 us
  waiting for transfers between devices  36.9 us (35%)
  starting transfers between devices  26.7 us (26%)
  blocking collectives  15.8 us (15%)
  Pallas kernels  13.8 us (13%)
  local copies, waits for them, and re-layouts  8.12 us (8%)
  other arithmetic  1.65 us (2%)
    all_to_all x1, starting transfers between devices, body(): incoming = lax.all_to_all(outgoing, 'ctx', 1, 0, tiled=True)  19.2 us
    all_to_all x1, waiting for transfers between devices, body(): incoming = lax.all_to_all(outgoing, 'ctx', 1, 0, tiled=True)  18.7 us
    all_to_all x1, waiting for transfers between devices, body(): conv = lax.all_to_all(conv, 'ctx', 1, 1, tiled=True).reshape(rows, channels)  18.2 us
    all_gather x1, blocking collectives, body(): total_sq = jnp.sum(lax.all_gather(squares, 'ch'), axis=0)  15.8 us
    pallas_call x1, Pallas kernels, causal_conv(): pl.pallas_call(lambda *refs: conv_kernel(width, *refs), out_shape=jax.Sha...  13.8 us
    all_to_all x1, starting transfers between devices, body(): conv = lax.all_to_all(conv, 'ctx', 1, 1, tiled=True).reshape(rows, channels)  7.49 us
  transfers between devices with their start and end apart: 2, of which 2 were waited for; matrix products, arithmetic and copies ran while one was open for 1% of the time, Pallas kernels for 0%

profile of v1, /device:TPU:1, one launch (start us, length us, event | category | flops | bytes accessed | tf_op | source)
XLA Modules:
  0.0 103.4 jit_solution(3462552187957802799)
XLA Ops:
  0.0 1.1 %copy.71 = bf16[128,512]{0,1:T(8,128)(2,1)S(1)} copy(bf16[128,512]{1,0:T(8,128)(2,1)} %param.8) | data formatting | bytes 262144 | tf_op args[1]
  1.1 0.0 copy-done
  1.1 0.1 copy.72
  1.2 0.0 copy-done.3
  1.2 0.1 copy.73
  1.3 0.1 copy.74
  1.5 0.2 copy.75
  1.7 0.1 broadcast_in_dim.31
  1.8 0.1 convert_element_type.31
  2.0 0.7 maximum_bitcast_fusion
  2.8 19.2 %all-to-all-start = ((bf16[160,64,8]{0,2,1:T(8,128)(2,1)}), bf16[160,64,8]{0,2,1:T(8,128)(2,1)S(1)}, u32[]{:S(2)}, u32[]{:S(2)}) async-start(bf16[160,64,8]{0,2,1:T(8,128)(2,1)} %maximum_bitcast_fusion), calls=%async_computation | async-start | bytes 524288 | tf_op jit(solution)/shard_map/all_to_all | solution.py:85
  22.0 0.0 copy-done.2
  22.1 0.3 select_reduce_fusion
  22.5 18.7 %all-to-all-done = bf16[160,64,8]{0,2,1:T(8,128)(2,1)S(1)} async-done(((bf16[160,64,8]{0,2,1:T(8,128)(2,1)}), bf16[160,64,8]{0,2,1:T(8,128)(2,1)S(1)}, u32[]{:S(2)}, u32[]{:S(2)}) %all-to-all-start) | async-done | bytes 163872 | tf_op jit(solution)/shard_map/all_to_all | solution.py:85
  41.2 0.3 copy.76
  41.6 0.1 copy.83
  41.7 0.1 copy.84
  41.8 0.8 rev.3.refs_0_
  42.6 0.2 copy.79
  42.8 0.6 gather_fusion
  43.5 0.8 copy.80.refs_1_
  44.2 13.8 %shard_map.73 = f32[128,512]{1,0:T(8,128)} custom-call(f32[64,256]{1,0:T(8,128)} %rev.3.refs_0_, bf16[128,512]{1,0:T(8,128)(2,1)} %copy.80.refs_1_), custom_call_target="tpu_custom_call" | custom-call | flops 2147483648 | bytes 458752 | tf_op jit(solution)/shard_map/pallas_call | solution.py:53
  58.1 1.1 %copy.81 = f32[128,512]{0,1:T(8,128)S(1)} copy(f32[128,512]{1,0:T(8,128)} %shard_map.73) | data formatting | bytes 524288 | tf_op jit(solution)/shard_map/pallas_call | solution.py:53
  59.2 1.3 %gather_fusion.1 = f32[64,128,8]{1,2,0:T(8,128)} fusion(f32[128,64,8]{0,2,1:T(8,128)S(1)} %bitcast.43, s32[1024]{0:T(1024)S(1)} %pad_clamp_fusion), kind=kCustom, calls=%fused_computation.1 | custom fusion | bytes 524544 | tf_op jit(solution)/shard_map/gather | solution.py:95
  60.5 7.5 %all-to-all-start.1 = ((f32[128,64,8]{0,2,1:T(8,128)}), f32[128,64,8]{0,2,1:T(8,128)S(1)}, u32[]{:S(2)}, u32[]{:S(2)}) async-start(f32[128,64,8]{0,2,1:T(8,128)} %bitcast.18), calls=%async_computation.1 | async-start | bytes 524288 | tf_op jit(solution)/shard_map/all_to_all | solution.py:96
  68.0 0.1 copy.70
  68.1 0.0 copy-start.5
  68.1 18.2 %all-to-all-done.1 = f32[128,64,8]{0,2,1:T(8,128)S(1)} async-done(((f32[128,64,8]{0,2,1:T(8,128)}), f32[128,64,8]{0,2,1:T(8,128)S(1)}, u32[]{:S(2)}, u32[]{:S(2)}) %all-to-all-start.1) | async-done | bytes 262176 | tf_op jit(solution)/shard_map/all_to_all | solution.py:96
  86.3 0.2 multiply_reduce_fusion
  86.5 15.8 %all-gather.1 = f32[8,1,128]{2,1,0:T(1,128)S(1)} all-gather(f32[1,1,128]{2,1,0:T(1,128)S(1)} %bitcast.52), channel_id=2, replica_groups=mesh['ctx'=64,'ch'=8] {'ch'}, dimensions={0}, use_global_device_ids=true | all-gather | bytes 4608 | tf_op jit(solution)/shard_map/all_gather | solution.py:101
  102.4 0.2 multiply_convert_fusion
  102.6 0.8 copy.82
  (25 shorter events, 0.3 us)
Async XLA Ops:
  0.0 1.1 %copy-start = (bf16[128,512]{1,0:T(8,128)(2,1)S(1)}, bf16[128,512]{1,0:T(8,128)(2,1)}, u32[]{:S(2)}) copy-start(bf16[128,512]{1,0:T(8,128)(2,1)} %param.9) | copy-start | bytes 393220
  0.0 1.2 %copy-start.3 = (f32[128,32]{0,1:T(8,128)S(1)}, f32[128,32]{0,1:T(8,128)}, u32[]{:S(2)}) copy-start(f32[128,32]{0,1:T(8,128)} %param.10) | copy-start | bytes 49156
  2.8 19.3 %copy-start.2 = (s32[2080,3]{0,1:T(4,128)S(1)}, s32[2080,3]{0,1:T(4,128)}, u32[]{:S(2)}) copy-start(s32[2080,3]{0,1:T(4,128)} %param.13) | copy-start | bytes 74884
  2.8 38.5 %all-to-all-start = ((bf16[160,64,8]{0,2,1:T(8,128)(2,1)}), bf16[160,64,8]{0,2,1:T(8,128)(2,1)S(1)}, u32[]{:S(2)}, u32[]{:S(2)}) async-start(bf16[160,64,8]{0,2,1:T(8,128)(2,1)} %maximum_bitcast_fusion), calls=%async_computation | async-start | bytes 524288 | tf_op jit(solution)/shard_map/all_to_all | solution.py:85
  60.5 7.5 %copy-start.1 = (bf16[128,512]{1,0:T(8,128)(2,1)S(1)}, bf16[128,512]{1,0:T(8,128)(2,1)}, u32[]{:S(2)}) copy-start(bf16[128,512]{1,0:T(8,128)(2,1)} %param.7) | copy-start | bytes 393220
  60.5 25.9 %copy-start.4 = (f32[512]{0:T(512)S(1)}, f32[512]{0:T(512)}, u32[]{:S(2)}) copy-start(f32[512]{0:T(512)} %param.11) | copy-start | bytes 6148
  60.5 25.9 %all-to-all-start.1 = ((f32[128,64,8]{0,2,1:T(8,128)}), f32[128,64,8]{0,2,1:T(8,128)S(1)}, u32[]{:S(2)}, u32[]{:S(2)}) async-start(f32[128,64,8]{0,2,1:T(8,128)} %bitcast.18), calls=%async_computation.1 | async-start | bytes 524288 | tf_op jit(solution)/shard_map/all_to_all | solution.py:96
  68.1 34.2 %copy-start.5 = (f32[512]{0:T(512)S(1)}, f32[512]{0:T(512)}, u32[]{:S(2)}) copy-start(f32[512]{0:T(512)} %param.12) | copy-start | bytes 6148

commit v2 on v1

--- a/solution.py
+++ b/solution.py
@@ -23,38 +23,37 @@
     return lax.reduce_precision(values, exponent_bits=8, mantissa_bits=7)
 
 
-def conv_kernel(width, window_ref, signal_ref, out_ref):
-    rows = out_ref.shape[0]
-    lanes = out_ref.shape[1]
+def conv_kernel(width, window_ref, signal_ref, out_ref, padded_ref):
+    rows = out_ref.shape[1]
+    lanes = out_ref.shape[0]
     blocks = window_ref.shape[0]
-    signal = signal_ref[...].astype(jnp.float32)
-    lane = lax.broadcasted_iota(jnp.int32, (rows, lanes), 1)
+    padded_ref[pl.ds(0, lanes), :] = jnp.zeros((lanes, rows), jnp.float32)
+    padded_ref[pl.ds(lanes, lanes), :] = signal_ref[...].astype(jnp.float32)
 
     def step(lag, total):
         window = jnp.broadcast_to(window_ref[pl.ds(lag, 1), :], (rows, 2 * rows))
-        skewed = pltpu.roll(window, rows + 1, 1, stride=1, stride_axis=0)
-        block = skewed[:, :rows]
+        block = pltpu.roll(window, rows, 1, stride=1, stride_axis=0)[:, :rows]
         block_hi = block.astype(jnp.bfloat16)
         block_lo = (block - block_hi.astype(jnp.float32)).astype(jnp.bfloat16)
-        moved = pltpu.roll(signal, lag * width, 1)
-        moved = jnp.where(lane >= lag * width, moved, 0.0).astype(jnp.bfloat16)
-        pair = jnp.concatenate([block_hi, block_lo], axis=1)
-        both = jnp.concatenate([moved, moved], axis=0)
-        return total + jnp.dot(pair, both, preferred_element_type=jnp.float32)
+        start = pl.multiple_of(lanes - lag * width, width)
+        moved = padded_ref[pl.ds(start, lanes), :].astype(jnp.bfloat16)
+        total = total + jnp.dot(moved, block_hi, preferred_element_type=jnp.float32)
+        return total + jnp.dot(moved, block_lo, preferred_element_type=jnp.float32)
 
     out_ref[...] = lax.fori_loop(
-        0, blocks, step, jnp.zeros((rows, lanes), jnp.float32), unroll=2
+        0, blocks, step, jnp.zeros((lanes, rows), jnp.float32), unroll=2
     )
 
 
 def causal_conv(window, signal, width):
-    rows, lanes = signal.shape
+    lanes, rows = signal.shape
     blocks = window.shape[0]
     return pl.pallas_call(
         lambda *refs: conv_kernel(width, *refs),
-        out_shape=jax.ShapeDtypeStruct((rows, lanes), jnp.float32),
+        out_shape=jax.ShapeDtypeStruct((lanes, rows), jnp.float32),
         in_specs=[pl.BlockSpec(memory_space=pltpu.VMEM)] * 2,
         out_specs=pl.BlockSpec(memory_space=pltpu.VMEM),
+        scratch_shapes=[pltpu.VMEM((2 * lanes, rows), jnp.float32)],
         cost_estimate=pl.CostEstimate(
             flops=4 * rows * rows * lanes * blocks,
             bytes_accessed=window.size * 4 + signal.size * 2 + rows * lanes * 4,
@@ -88,12 +87,13 @@
     taps_in = incoming[:, rows:, :].astype(jnp.float32).reshape(blocks, 2, rows)
     my_taps = taps_in[:, 0, :] + taps_in[:, 1, :]
     earlier = jnp.concatenate([jnp.zeros((1, rows), jnp.float32), my_taps[:-1]], axis=0)
-    window = jnp.concatenate([earlier, my_taps], axis=1)[:, ::-1]
+    window = jnp.concatenate([earlier, my_taps], axis=1)
 
-    lined = in_order.transpose(1, 0, 2).reshape(rows, blocks * width)
+    lined = in_order.transpose(0, 2, 1).reshape(blocks * width, rows)
     conv = causal_conv(window, lined, width)
-    conv = conv.reshape(rows, blocks, width)[:, holder, :]
-    conv = lax.all_to_all(conv, "ctx", 1, 1, tiled=True).reshape(rows, channels)
+    conv = conv.reshape(blocks, width, rows)[holder]
+    conv = lax.all_to_all(conv, "ctx", 0, 0, tiled=True)
+    conv = conv.transpose(2, 0, 1).reshape(rows, channels)
 
     long_conv = conv + conv_bias[None, :] * product
     gated = query.astype(jnp.float32) * long_conv

time: 104 us -> 104 us (level)
  local copies, waits for them, and re-layouts: 8.12 us -> 7.04 us
    pallas_call x1 -> x0, local copies, waits for them, and re-layouts: 1.07 us -> none  [causal_conv(): pl.pallas_call(lambda *refs: conv_kernel(width, *refs), out_shape=jax.Sha...]
where the time goes in v2:
time: 104 us
  waiting for transfers between devices  36.9 us (35%)
  starting transfers between devices  26.7 us (26%)
  blocking collectives  15.8 us (15%)
  Pallas kernels  14.8 us (14%)
  local copies, waits for them, and re-layouts  7.04 us (7%)
  other arithmetic  2.26 us (2%)
    all_to_all x1, starting transfers between devices, body(): incoming = lax.all_to_all(outgoing, 'ctx', 1, 0, tiled=True)  19.2 us
    all_to_all x1, waiting for transfers between devices, body(): incoming = lax.all_to_all(outgoing, 'ctx', 1, 0, tiled=True)  18.7 us
    all_to_all x1, waiting for transfers between devices, body(): conv = lax.all_to_all(conv, 'ctx', 0, 0, tiled=True)  18.2 us
    all_gather x1, blocking collectives, body(): total_sq = jnp.sum(lax.all_gather(squares, 'ch'), axis=0)  15.8 us
    pallas_call x1, Pallas kernels, causal_conv(): pl.pallas_call(lambda *refs: conv_kernel(width, *refs), out_shape=jax.Sha...  14.8 us
    all_to_all x1, starting transfers between devices, body(): conv = lax.all_to_all(conv, 'ctx', 0, 0, tiled=True)  7.49 us
    gather x1, local copies, waits for them, and re-layouts, body(): conv = conv.reshape(blocks, width, rows)[holder]  2.24 us
  transfers between devices with their start and end apart: 2, of which 2 were waited for; matrix products, arithmetic and copies ran while one was open for 1% of the time, Pallas kernels for 0%

profile of v2, /device:TPU:1, one launch (start us, length us, event | category | flops | bytes accessed | tf_op | source)
XLA Modules:
  0.0 103.8 jit_solution(8465548744169986812)
XLA Ops:
  0.0 1.1 %copy.62 = bf16[128,512]{0,1:T(8,128)(2,1)S(1)} copy(bf16[128,512]{1,0:T(8,128)(2,1)} %param.8) | data formatting | bytes 262144 | tf_op args[1]
  1.1 0.0 copy-done
  1.1 0.1 copy.63
  1.2 0.0 copy-done.3
  1.2 0.1 copy.64
  1.3 0.1 copy.65
  1.5 0.2 copy.66
  1.7 0.1 broadcast_in_dim.31
  1.8 0.1 convert_element_type.31
  2.0 0.7 maximum_bitcast_fusion
  2.8 19.2 %all-to-all-start = ((bf16[160,64,8]{0,2,1:T(8,128)(2,1)}), bf16[160,64,8]{0,2,1:T(8,128)(2,1)S(1)}, u32[]{:S(2)}, u32[]{:S(2)}) async-start(bf16[160,64,8]{0,2,1:T(8,128)(2,1)} %maximum_bitcast_fusion), calls=%async_computation | async-start | bytes 524288 | tf_op jit(solution)/shard_map/all_to_all | solution.py:84
  22.1 0.3 select_reduce_fusion
  22.5 18.7 %all-to-all-done = bf16[160,64,8]{0,2,1:T(8,128)(2,1)S(1)} async-done(((bf16[160,64,8]{0,2,1:T(8,128)(2,1)}), bf16[160,64,8]{0,2,1:T(8,128)(2,1)S(1)}, u32[]{:S(2)}, u32[]{:S(2)}) %all-to-all-start) | async-done | bytes 163872 | tf_op jit(solution)/shard_map/all_to_all | solution.py:84
  41.2 0.3 copy.67
  41.6 0.1 copy.72
  41.7 0.1 copy.73
  41.8 0.2 copy.70
  42.0 0.6 select_maximum_fusion.refs_0_
  42.6 1.3 %gather_fusion = bf16[64,128,8]{1,2,0:T(8,128)(2,1)} fusion(bf16[64,128,8]{1,2,0:T(8,128)(2,1)S(1)} %copy.70, s32[1024]{0:T(1024)S(1)} %pad_clamp_fusion.1), kind=kCustom, calls=%fused_computation | custom fusion | bytes 262400 | tf_op jit(solution)/shard_map/gather | solution.py:86
  43.9 14.8 %shard_map.73 = f32[512,128]{1,0:T(8,128)} custom-call(f32[64,256]{1,0:T(8,128)} %select_maximum_fusion.refs_0_, bf16[512,128]{1,0:T(8,128)(2,1)} %bitcast.44), custom_call_target="tpu_custom_call" | custom-call | flops 2147483648 | bytes 458752 | tf_op jit(solution)/shard_map/pallas_call | solution.py:51
  58.7 2.2 %gather_fusion.1 = f32[64,8,128]{2,1,0:T(8,128)} fusion(f32[64,8,128]{2,1,0:T(8,128)} %bitcast.49, s32[1024]{0:T(1024)S(1)} %pad_clamp_fusion), kind=kCustom, calls=%fused_computation.1 | custom fusion | bytes 524544 | tf_op jit(solution)/shard_map/gather | solution.py:94
  60.9 7.5 %all-to-all-start.1 = ((f32[64,8,128]{2,1,0:T(8,128)}), f32[64,8,128]{2,1,0:T(8,128)S(1)}, u32[]{:S(2)}, u32[]{:S(2)}) async-start(f32[64,8,128]{2,1,0:T(8,128)} %gather_fusion.1), calls=%async_computation.1 | async-start | bytes 524288 | tf_op jit(solution)/shard_map/all_to_all | solution.py:95
  68.4 0.0 copy-done.1
  68.5 0.1 copy.61
  68.6 0.0 copy-start.5
  68.6 18.2 %all-to-all-done.1 = f32[64,8,128]{2,1,0:T(8,128)S(1)} async-done(((f32[64,8,128]{2,1,0:T(8,128)}), f32[64,8,128]{2,1,0:T(8,128)S(1)}, u32[]{:S(2)}, u32[]{:S(2)}) %all-to-all-start.1) | async-done | bytes 262176 | tf_op jit(solution)/shard_map/all_to_all | solution.py:95
  86.8 0.0 copy-done.4
  86.8 0.2 multiply_reduce_fusion
  87.0 15.8 %all-gather.1 = f32[8,1,128]{2,1,0:T(1,128)S(1)} all-gather(f32[1,1,128]{2,1,0:T(1,128)S(1)} %bitcast.53), channel_id=2, replica_groups=mesh['ctx'=64,'ch'=8] {'ch'}, dimensions={0}, use_global_device_ids=true | all-gather | bytes 4608 | tf_op jit(solution)/shard_map/all_gather | solution.py:101
  102.8 0.0 copy-done.5
  102.8 0.2 multiply_convert_fusion
  103.0 0.8 copy.71
  (22 shorter events, 0.3 us)
Async XLA Ops:
  0.0 1.1 %copy-start = (bf16[128,512]{1,0:T(8,128)(2,1)S(1)}, bf16[128,512]{1,0:T(8,128)(2,1)}, u32[]{:S(2)}) copy-start(bf16[128,512]{1,0:T(8,128)(2,1)} %param.9) | copy-start | bytes 393220
  0.0 1.2 %copy-start.3 = (f32[128,32]{0,1:T(8,128)S(1)}, f32[128,32]{0,1:T(8,128)}, u32[]{:S(2)}) copy-start(f32[128,32]{0,1:T(8,128)} %param.10) | copy-start | bytes 49156
  2.8 19.3 %copy-start.2 = (s32[2080,3]{0,1:T(4,128)S(1)}, s32[2080,3]{0,1:T(4,128)}, u32[]{:S(2)}) copy-start(s32[2080,3]{0,1:T(4,128)} %param.13) | copy-start | bytes 74884
  2.8 38.5 %all-to-all-start = ((bf16[160,64,8]{0,2,1:T(8,128)(2,1)}), bf16[160,64,8]{0,2,1:T(8,128)(2,1)S(1)}, u32[]{:S(2)}, u32[]{:S(2)}) async-start(bf16[160,64,8]{0,2,1:T(8,128)(2,1)} %maximum_bitcast_fusion), calls=%async_computation | async-start | bytes 524288 | tf_op jit(solution)/shard_map/all_to_all | solution.py:84
  60.9 7.5 %copy-start.1 = (bf16[128,512]{1,0:T(8,128)(2,1)S(1)}, bf16[128,512]{1,0:T(8,128)(2,1)}, u32[]{:S(2)}) copy-start(bf16[128,512]{1,0:T(8,128)(2,1)} %param.7) | copy-start | bytes 393220
  60.9 25.9 %copy-start.4 = (f32[512]{0:T(512)S(1)}, f32[512]{0:T(512)}, u32[]{:S(2)}) copy-start(f32[512]{0:T(512)} %param.11) | copy-start | bytes 6148
  60.9 25.9 %all-to-all-start.1 = ((f32[64,8,128]{2,1,0:T(8,128)}), f32[64,8,128]{2,1,0:T(8,128)S(1)}, u32[]{:S(2)}, u32[]{:S(2)}) async-start(f32[64,8,128]{2,1,0:T(8,128)} %gather_fusion.1), calls=%async_computation.1 | async-start | bytes 524288 | tf_op jit(solution)/shard_map/all_to_all | solution.py:95
  68.6 34.2 %copy-start.5 = (f32[512]{0:T(512)S(1)}, f32[512]{0:T(512)}, u32[]{:S(2)}) copy-start(f32[512]{0:T(512)} %param.12) | copy-start | bytes 6148

commit v3 on v2

--- a/solution.py
+++ b/solution.py
@@ -85,13 +85,15 @@
     incoming = incoming.reshape(blocks, rows + 2 * rows // width, width)
     in_order = incoming[:, :rows, :][device_of]
     taps_in = incoming[:, rows:, :].astype(jnp.float32).reshape(blocks, 2, rows)
-    my_taps = taps_in[:, 0, :] + taps_in[:, 1, :]
-    earlier = jnp.concatenate([jnp.zeros((1, rows), jnp.float32), my_taps[:-1]], axis=0)
+    span = 2 * rows
+    wide = blocks // 2
+    my_taps = (taps_in[:, 0, :] + taps_in[:, 1, :]).reshape(wide, span)
+    earlier = jnp.concatenate([jnp.zeros((1, span), jnp.float32), my_taps[:-1]], axis=0)
     window = jnp.concatenate([earlier, my_taps], axis=1)
 
-    lined = in_order.transpose(0, 2, 1).reshape(blocks * width, rows)
+    lined = in_order.reshape(wide, span, width).transpose(0, 2, 1).reshape(wide * width, span)
     conv = causal_conv(window, lined, width)
-    conv = conv.reshape(blocks, width, rows)[holder]
+    conv = conv.reshape(wide, width, 2, rows).transpose(0, 2, 1, 3).reshape(blocks, width, rows)[holder]
     conv = lax.all_to_all(conv, "ctx", 0, 0, tiled=True)
     conv = conv.transpose(2, 0, 1).reshape(rows, channels)
 

time: 104 us -> 98.8 us (0.950)
  Pallas kernels: 14.8 us -> 9.41 us
    pallas_call x1, Pallas kernels: 14.8 us -> 9.41 us  [causal_conv(): pl.pallas_call(lambda *refs: conv_kernel(width, *refs), out_shape=jax.Sha...]
where the time goes in v3:
time: 98.8 us; the launch traced here: 98.5 us
  waiting for transfers between devices  36.9 us (37%)
  starting transfers between devices  26.7 us (27%)
  blocking collectives  15.8 us (16%)
  Pallas kernels  9.41 us (10%)
  local copies, waits for them, and re-layouts  7.07 us (7%)
  other arithmetic  2.25 us (2%)
    all_to_all x1, starting transfers between devices, body(): incoming = lax.all_to_all(outgoing, 'ctx', 1, 0, tiled=True)  19.2 us
    all_to_all x1, waiting for transfers between devices, body(): incoming = lax.all_to_all(outgoing, 'ctx', 1, 0, tiled=True)  18.7 us
    all_to_all x1, waiting for transfers between devices, body(): conv = lax.all_to_all(conv, 'ctx', 0, 0, tiled=True)  18.2 us
    all_gather x1, blocking collectives, body(): total_sq = jnp.sum(lax.all_gather(squares, 'ch'), axis=0)  15.8 us
    pallas_call x1, Pallas kernels, causal_conv(): pl.pallas_call(lambda *refs: conv_kernel(width, *refs), out_shape=jax.Sha...  9.41 us
    all_to_all x1, starting transfers between devices, body(): conv = lax.all_to_all(conv, 'ctx', 0, 0, tiled=True)  7.49 us
    gather x1, local copies, waits for them, and re-layouts, body(): conv.reshape(wide, width, 2, rows).transpose(0, 2, 1, 3)  2.24 us
  transfers between devices with their start and end apart: 2, of which 2 were waited for; matrix products, arithmetic and copies ran while one was open for 1% of the time, Pallas kernels for 0%

profile of v3, /device:TPU:1, one launch (start us, length us, event | category | flops | bytes accessed | tf_op | source)
XLA Modules:
  0.0 98.5 jit_solution(13276675698530334818)
XLA Ops:
  0.0 1.1 %copy.61 = bf16[128,512]{0,1:T(8,128)(2,1)S(1)} copy(bf16[128,512]{1,0:T(8,128)(2,1)} %param.8) | data formatting | bytes 262144 | tf_op args[1]
  1.1 0.0 copy-done
  1.1 0.1 copy.62
  1.2 0.0 copy-done.3
  1.2 0.1 copy.63
  1.3 0.1 copy.64
  1.5 0.2 copy.65
  1.7 0.1 broadcast_in_dim.31
  1.8 0.1 convert_element_type.31
  2.0 0.7 maximum_bitcast_fusion
  2.8 19.2 %all-to-all-start = ((bf16[160,64,8]{0,2,1:T(8,128)(2,1)}), bf16[160,64,8]{0,2,1:T(8,128)(2,1)S(1)}, u32[]{:S(2)}, u32[]{:S(2)}) async-start(bf16[160,64,8]{0,2,1:T(8,128)(2,1)} %maximum_bitcast_fusion), calls=%async_computation | async-start | bytes 524288 | tf_op jit(solution)/shard_map/all_to_all | solution.py:84
  22.0 0.0 copy-done.2
  22.1 0.3 select_reduce_fusion
  22.5 18.7 %all-to-all-done = bf16[160,64,8]{0,2,1:T(8,128)(2,1)S(1)} async-done(((bf16[160,64,8]{0,2,1:T(8,128)(2,1)}), bf16[160,64,8]{0,2,1:T(8,128)(2,1)S(1)}, u32[]{:S(2)}, u32[]{:S(2)}) %all-to-all-start) | async-done | bytes 163872 | tf_op jit(solution)/shard_map/all_to_all | solution.py:84
  41.2 0.3 copy.66
  41.6 0.1 copy.68
  41.7 0.1 copy.67
  41.8 0.2 copy.69
  42.0 0.6 select_maximum_fusion.refs_0_
  42.7 1.3 %gather_fusion = bf16[64,128,8]{1,2,0:T(8,128)(2,1)} fusion(bf16[64,128,8]{1,2,0:T(8,128)(2,1)S(1)} %copy.69, s32[1024]{0:T(1024)S(1)} %pad_clamp_fusion.1), kind=kCustom, calls=%fused_computation | custom fusion | bytes 262400 | tf_op jit(solution)/shard_map/gather | solution.py:86
  43.9 9.4 %shard_map.73 = f32[256,256]{1,0:T(8,128)} custom-call(f32[32,512]{1,0:T(8,128)} %select_maximum_fusion.refs_0_, bf16[256,256]{1,0:T(8,128)(2,1)} %bitcast.52), custom_call_target="tpu_custom_call" | custom-call | flops 2147483648 | bytes 458752 | tf_op jit(solution)/shard_map/pallas_call | solution.py:51
  53.3 2.2 %gather_fusion.1 = f32[64,8,128]{2,1,0:T(8,128)} fusion(f32[64,8,128]{2,1,0:T(8,128)} %bitcast.57, s32[1024]{0:T(1024)S(1)} %pad_clamp_fusion), kind=kCustom, calls=%fused_computation.1 | custom fusion | bytes 524544 | tf_op jit(solution)/shard_map/gather | solution.py:96
  55.6 7.5 %all-to-all-start.1 = ((f32[64,8,128]{2,1,0:T(8,128)}), f32[64,8,128]{2,1,0:T(8,128)S(1)}, u32[]{:S(2)}, u32[]{:S(2)}) async-start(f32[64,8,128]{2,1,0:T(8,128)} %gather_fusion.1), calls=%async_computation.1 | async-start | bytes 524288 | tf_op jit(solution)/shard_map/all_to_all | solution.py:97
  63.1 0.0 copy-done.1
  63.1 0.1 copy.60
  63.2 0.0 copy-start.5
  63.2 18.2 %all-to-all-done.1 = f32[64,8,128]{2,1,0:T(8,128)S(1)} async-done(((f32[64,8,128]{2,1,0:T(8,128)}), f32[64,8,128]{2,1,0:T(8,128)S(1)}, u32[]{:S(2)}, u32[]{:S(2)}) %all-to-all-start.1) | async-done | bytes 262176 | tf_op jit(solution)/shard_map/all_to_all | solution.py:97
  81.5 0.0 copy-done.4
  81.5 0.2 multiply_reduce_fusion
  81.6 15.8 %all-gather.1 = f32[8,1,128]{2,1,0:T(1,128)S(1)} all-gather(f32[1,1,128]{2,1,0:T(1,128)S(1)} %bitcast.61), channel_id=2, replica_groups=mesh['ctx'=64,'ch'=8] {'ch'}, dimensions={0}, use_global_device_ids=true | all-gather | bytes 4608 | tf_op jit(solution)/shard_map/all_gather | solution.py:103
  97.5 0.2 multiply_convert_fusion
  97.7 0.8 copy.70
  (22 shorter events, 0.3 us)
Async XLA Ops:
  0.0 1.1 %copy-start = (bf16[128,512]{1,0:T(8,128)(2,1)S(1)}, bf16[128,512]{1,0:T(8,128)(2,1)}, u32[]{:S(2)}) copy-start(bf16[128,512]{1,0:T(8,128)(2,1)} %param.9) | copy-start | bytes 393220
  0.0 1.2 %copy-start.3 = (f32[128,32]{0,1:T(8,128)S(1)}, f32[128,32]{0,1:T(8,128)}, u32[]{:S(2)}) copy-start(f32[128,32]{0,1:T(8,128)} %param.10) | copy-start | bytes 49156
  2.8 19.3 %copy-start.2 = (s32[2080,3]{0,1:T(4,128)S(1)}, s32[2080,3]{0,1:T(4,128)}, u32[]{:S(2)}) copy-start(s32[2080,3]{0,1:T(4,128)} %param.13) | copy-start | bytes 74884
  2.8 38.5 %all-to-all-start = ((bf16[160,64,8]{0,2,1:T(8,128)(2,1)}), bf16[160,64,8]{0,2,1:T(8,128)(2,1)S(1)}, u32[]{:S(2)}, u32[]{:S(2)}) async-start(bf16[160,64,8]{0,2,1:T(8,128)(2,1)} %maximum_bitcast_fusion), calls=%async_computation | async-start | bytes 524288 | tf_op jit(solution)/shard_map/all_to_all | solution.py:84
  55.6 7.5 %copy-start.1 = (bf16[128,512]{1,0:T(8,128)(2,1)S(1)}, bf16[128,512]{1,0:T(8,128)(2,1)}, u32[]{:S(2)}) copy-start(bf16[128,512]{1,0:T(8,128)(2,1)} %param.7) | copy-start | bytes 393220
  55.6 25.9 %copy-start.4 = (f32[512]{0:T(512)S(1)}, f32[512]{0:T(512)}, u32[]{:S(2)}) copy-start(f32[512]{0:T(512)} %param.11) | copy-start | bytes 6148
  55.6 25.9 %all-to-all-start.1 = ((f32[64,8,128]{2,1,0:T(8,128)}), f32[64,8,128]{2,1,0:T(8,128)S(1)}, u32[]{:S(2)}, u32[]{:S(2)}) async-start(f32[64,8,128]{2,1,0:T(8,128)} %gather_fusion.1), calls=%async_computation.1 | async-start | bytes 524288 | tf_op jit(solution)/shard_map/all_to_all | solution.py:97
  63.2 34.3 %copy-start.5 = (f32[512]{0:T(512)S(1)}, f32[512]{0:T(512)}, u32[]{:S(2)}) copy-start(f32[512]{0:T(512)} %param.12) | copy-start | bytes 6148

commit v4 on v3

--- a/solution.py
+++ b/solution.py
@@ -30,18 +30,30 @@
     padded_ref[pl.ds(0, lanes), :] = jnp.zeros((lanes, rows), jnp.float32)
     padded_ref[pl.ds(lanes, lanes), :] = signal_ref[...].astype(jnp.float32)
 
-    def step(lag, total):
+    half = lanes // 2
+
+    def lag_block(lag):
         window = jnp.broadcast_to(window_ref[pl.ds(lag, 1), :], (rows, 2 * rows))
         block = pltpu.roll(window, rows, 1, stride=1, stride_axis=0)[:, :rows]
         block_hi = block.astype(jnp.bfloat16)
         block_lo = (block - block_hi.astype(jnp.float32)).astype(jnp.bfloat16)
-        start = pl.multiple_of(lanes - lag * width, width)
-        moved = padded_ref[pl.ds(start, lanes), :].astype(jnp.bfloat16)
+        return block_hi, block_lo
+
+    def add_lag(total, lag, offset, count):
+        block_hi, block_lo = lag_block(lag)
+        start = pl.multiple_of(lanes - lag * width + offset, width)
+        moved = padded_ref[pl.ds(start, count), :].astype(jnp.bfloat16)
         total = total + jnp.dot(moved, block_hi, preferred_element_type=jnp.float32)
         return total + jnp.dot(moved, block_lo, preferred_element_type=jnp.float32)
 
-    out_ref[...] = lax.fori_loop(
-        0, blocks, step, jnp.zeros((lanes, rows), jnp.float32), unroll=2
+    total = lax.fori_loop(
+        0, blocks // 2, lambda lag, acc: add_lag(acc, lag, 0, lanes),
+        jnp.zeros((lanes, rows), jnp.float32), unroll=2,
+    )
+    out_ref[pl.ds(0, half), :] = total[:half]
+    out_ref[pl.ds(half, half), :] = lax.fori_loop(
+        blocks // 2, blocks, lambda lag, acc: add_lag(acc, lag, half, half),
+        total[half:], unroll=2,
     )
 
 

time: 98.8 us -> 98.2 us (level)
  no operation moved by 1% of the time
where the time goes in v4:
time: 98.2 us; the launch traced here: 97.8 us
  waiting for transfers between devices  36.9 us (38%)
  starting transfers between devices  26.7 us (27%)
  blocking collectives  15.8 us (16%)
  Pallas kernels  8.83 us (9%)
  local copies, waits for them, and re-layouts  7.07 us (7%)
  other arithmetic  2.25 us (2%)
    all_to_all x1, starting transfers between devices, body(): incoming = lax.all_to_all(outgoing, 'ctx', 1, 0, tiled=True)  19.2 us
    all_to_all x1, waiting for transfers between devices, body(): incoming = lax.all_to_all(outgoing, 'ctx', 1, 0, tiled=True)  18.7 us
    all_to_all x1, waiting for transfers between devices, body(): conv = lax.all_to_all(conv, 'ctx', 0, 0, tiled=True)  18.2 us
    all_gather x1, blocking collectives, body(): total_sq = jnp.sum(lax.all_gather(squares, 'ch'), axis=0)  15.8 us
    pallas_call x1, Pallas kernels, causal_conv(): pl.pallas_call(lambda *refs: conv_kernel(width, *refs), out_shape=jax.Sha...  8.83 us
    all_to_all x1, starting transfers between devices, body(): conv = lax.all_to_all(conv, 'ctx', 0, 0, tiled=True)  7.5 us
    gather x1, local copies, waits for them, and re-layouts, body(): conv.reshape(wide, width, 2, rows).transpose(0, 2, 1, 3)  2.24 us
  transfers between devices with their start and end apart: 2, of which 2 were waited for; matrix products, arithmetic and copies ran while one was open for 1% of the time, Pallas kernels for 0%

profile of v4, /device:TPU:1, one launch (start us, length us, event | category | flops | bytes accessed | tf_op | source)
XLA Modules:
  0.0 97.8 jit_solution(5277026869531326120)
XLA Ops:
  0.0 1.1 %copy.61 = bf16[128,512]{0,1:T(8,128)(2,1)S(1)} copy(bf16[128,512]{1,0:T(8,128)(2,1)} %param.8) | data formatting | bytes 262144 | tf_op args[1]
  1.1 0.0 copy-done
  1.1 0.1 copy.62
  1.2 0.0 copy-done.3
  1.2 0.1 copy.63
  1.3 0.1 copy.64
  1.5 0.2 copy.65
  1.7 0.1 broadcast_in_dim.31
  1.8 0.1 convert_element_type.31
  2.0 0.7 maximum_bitcast_fusion
  2.8 19.2 %all-to-all-start = ((bf16[160,64,8]{0,2,1:T(8,128)(2,1)}), bf16[160,64,8]{0,2,1:T(8,128)(2,1)S(1)}, u32[]{:S(2)}, u32[]{:S(2)}) async-start(bf16[160,64,8]{0,2,1:T(8,128)(2,1)} %maximum_bitcast_fusion), calls=%async_computation | async-start | bytes 524288 | tf_op jit(solution)/shard_map/all_to_all | solution.py:96
  22.0 0.0 copy-done.2
  22.1 0.3 select_reduce_fusion
  22.5 18.7 %all-to-all-done = bf16[160,64,8]{0,2,1:T(8,128)(2,1)S(1)} async-done(((bf16[160,64,8]{0,2,1:T(8,128)(2,1)}), bf16[160,64,8]{0,2,1:T(8,128)(2,1)S(1)}, u32[]{:S(2)}, u32[]{:S(2)}) %all-to-all-start) | async-done | bytes 163872 | tf_op jit(solution)/shard_map/all_to_all | solution.py:96
  41.2 0.3 copy.66
  41.6 0.1 copy.68
  41.7 0.1 copy.67
  41.8 0.2 copy.69
  42.0 0.6 select_maximum_fusion.refs_0_
  42.7 1.3 %gather_fusion = bf16[64,128,8]{1,2,0:T(8,128)(2,1)} fusion(bf16[64,128,8]{1,2,0:T(8,128)(2,1)S(1)} %copy.69, s32[1024]{0:T(1024)S(1)} %pad_clamp_fusion.1), kind=kCustom, calls=%fused_computation | custom fusion | bytes 262400 | tf_op jit(solution)/shard_map/gather | solution.py:98
  43.9 8.8 %shard_map.73 = f32[256,256]{1,0:T(8,128)} custom-call(f32[32,512]{1,0:T(8,128)} %select_maximum_fusion.refs_0_, bf16[256,256]{1,0:T(8,128)(2,1)} %bitcast.52), custom_call_target="tpu_custom_call" | custom-call | flops 2147483648 | bytes 458752 | tf_op jit(solution)/shard_map/pallas_call | solution.py:63
  52.8 2.2 %gather_fusion.1 = f32[64,8,128]{2,1,0:T(8,128)} fusion(f32[64,8,128]{2,1,0:T(8,128)} %bitcast.57, s32[1024]{0:T(1024)S(1)} %pad_clamp_fusion), kind=kCustom, calls=%fused_computation.1 | custom fusion | bytes 524544 | tf_op jit(solution)/shard_map/gather | solution.py:108
  55.0 7.5 %all-to-all-start.1 = ((f32[64,8,128]{2,1,0:T(8,128)}), f32[64,8,128]{2,1,0:T(8,128)S(1)}, u32[]{:S(2)}, u32[]{:S(2)}) async-start(f32[64,8,128]{2,1,0:T(8,128)} %gather_fusion.1), calls=%async_computation.1 | async-start | bytes 524288 | tf_op jit(solution)/shard_map/all_to_all | solution.py:109
  62.5 0.0 copy-done.1
  62.5 0.1 copy.60
  62.7 0.0 copy-start.5
  62.7 18.2 %all-to-all-done.1 = f32[64,8,128]{2,1,0:T(8,128)S(1)} async-done(((f32[64,8,128]{2,1,0:T(8,128)}), f32[64,8,128]{2,1,0:T(8,128)S(1)}, u32[]{:S(2)}, u32[]{:S(2)}) %all-to-all-start.1) | async-done | bytes 262176 | tf_op jit(solution)/shard_map/all_to_all | solution.py:109
  80.9 0.0 copy-done.4
  80.9 0.2 multiply_reduce_fusion
  81.0 15.8 %all-gather.1 = f32[8,1,128]{2,1,0:T(1,128)S(1)} all-gather(f32[1,1,128]{2,1,0:T(1,128)S(1)} %bitcast.61), channel_id=2, replica_groups=mesh['ctx'=64,'ch'=8] {'ch'}, dimensions={0}, use_global_device_ids=true | all-gather | bytes 4608 | tf_op jit(solution)/shard_map/all_gather | solution.py:115
  96.9 0.2 multiply_convert_fusion
  97.1 0.8 copy.70
  (22 shorter events, 0.3 us)
Async XLA Ops:
  0.0 1.1 %copy-start = (bf16[128,512]{1,0:T(8,128)(2,1)S(1)}, bf16[128,512]{1,0:T(8,128)(2,1)}, u32[]{:S(2)}) copy-start(bf16[128,512]{1,0:T(8,128)(2,1)} %param.9) | copy-start | bytes 393220
  0.0 1.2 %copy-start.3 = (f32[128,32]{0,1:T(8,128)S(1)}, f32[128,32]{0,1:T(8,128)}, u32[]{:S(2)}) copy-start(f32[128,32]{0,1:T(8,128)} %param.10) | copy-start | bytes 49156
  2.8 19.3 %copy-start.2 = (s32[2080,3]{0,1:T(4,128)S(1)}, s32[2080,3]{0,1:T(4,128)}, u32[]{:S(2)}) copy-start(s32[2080,3]{0,1:T(4,128)} %param.13) | copy-start | bytes 74884
  2.8 38.5 %all-to-all-start = ((bf16[160,64,8]{0,2,1:T(8,128)(2,1)}), bf16[160,64,8]{0,2,1:T(8,128)(2,1)S(1)}, u32[]{:S(2)}, u32[]{:S(2)}) async-start(bf16[160,64,8]{0,2,1:T(8,128)(2,1)} %maximum_bitcast_fusion), calls=%async_computation | async-start | bytes 524288 | tf_op jit(solution)/shard_map/all_to_all | solution.py:96
  55.0 7.5 %copy-start.1 = (bf16[128,512]{1,0:T(8,128)(2,1)S(1)}, bf16[128,512]{1,0:T(8,128)(2,1)}, u32[]{:S(2)}) copy-start(bf16[128,512]{1,0:T(8,128)(2,1)} %param.7) | copy-start | bytes 393220
  55.0 25.9 %copy-start.4 = (f32[512]{0:T(512)S(1)}, f32[512]{0:T(512)}, u32[]{:S(2)}) copy-start(f32[512]{0:T(512)} %param.11) | copy-start | bytes 6148
  55.0 25.9 %all-to-all-start.1 = ((f32[64,8,128]{2,1,0:T(8,128)}), f32[64,8,128]{2,1,0:T(8,128)S(1)}, u32[]{:S(2)}, u32[]{:S(2)}) async-start(f32[64,8,128]{2,1,0:T(8,128)} %gather_fusion.1), calls=%async_computation.1 | async-start | bytes 524288 | tf_op jit(solution)/shard_map/all_to_all | solution.py:109
  62.7 34.2 %copy-start.5 = (f32[512]{0:T(512)S(1)}, f32[512]{0:T(512)}, u32[]{:S(2)}) copy-start(f32[512]{0:T(512)} %param.12) | copy-start | bytes 6148

commit v5 on v4

--- a/solution.py
+++ b/solution.py
@@ -26,40 +26,38 @@
 def conv_kernel(width, window_ref, signal_ref, out_ref, padded_ref):
     rows = out_ref.shape[1]
     lanes = out_ref.shape[0]
-    blocks = window_ref.shape[0]
+    pairs = window_ref.shape[0]
+    half = lanes // 2
     padded_ref[pl.ds(0, lanes), :] = jnp.zeros((lanes, rows), jnp.float32)
     padded_ref[pl.ds(lanes, lanes), :] = signal_ref[...].astype(jnp.float32)
 
-    half = lanes // 2
-
-    def lag_block(lag):
-        window = jnp.broadcast_to(window_ref[pl.ds(lag, 1), :], (rows, 2 * rows))
-        block = pltpu.roll(window, rows, 1, stride=1, stride_axis=0)[:, :rows]
+    def add_lag(total, block, lag, offset, count):
         block_hi = block.astype(jnp.bfloat16)
         block_lo = (block - block_hi.astype(jnp.float32)).astype(jnp.bfloat16)
-        return block_hi, block_lo
-
-    def add_lag(total, lag, offset, count):
-        block_hi, block_lo = lag_block(lag)
         start = pl.multiple_of(lanes - lag * width + offset, width)
         moved = padded_ref[pl.ds(start, count), :].astype(jnp.bfloat16)
         total = total + jnp.dot(moved, block_hi, preferred_element_type=jnp.float32)
         return total + jnp.dot(moved, block_lo, preferred_element_type=jnp.float32)
 
+    def add_pair(total, pair, offset, count):
+        window = jnp.broadcast_to(window_ref[pl.ds(pair, 1), :], (rows, 3 * rows))
+        skewed = pltpu.roll(window, 2 * rows, 1, stride=1, stride_axis=0)
+        total = add_lag(total, skewed[:, :rows], 2 * pair, offset, count)
+        return add_lag(total, skewed[:, rows : 2 * rows], 2 * pair + 1, offset, count)
+
     total = lax.fori_loop(
-        0, blocks // 2, lambda lag, acc: add_lag(acc, lag, 0, lanes),
-        jnp.zeros((lanes, rows), jnp.float32), unroll=2,
+        0, pairs // 2, lambda pair, acc: add_pair(acc, pair, 0, lanes),
+        jnp.zeros((lanes, rows), jnp.float32),
     )
     out_ref[pl.ds(0, half), :] = total[:half]
     out_ref[pl.ds(half, half), :] = lax.fori_loop(
-        blocks // 2, blocks, lambda lag, acc: add_lag(acc, lag, half, half),
-        total[half:], unroll=2,
+        pairs // 2, pairs, lambda pair, acc: add_pair(acc, pair, half, half), total[half:],
     )
 
 
 def causal_conv(window, signal, width):
     lanes, rows = signal.shape
-    blocks = window.shape[0]
+    blocks = 2 * window.shape[0]
     return pl.pallas_call(
         lambda *refs: conv_kernel(width, *refs),
         out_shape=jax.ShapeDtypeStruct((lanes, rows), jnp.float32),
@@ -100,8 +98,8 @@
     span = 2 * rows
     wide = blocks // 2
     my_taps = (taps_in[:, 0, :] + taps_in[:, 1, :]).reshape(wide, span)
-    earlier = jnp.concatenate([jnp.zeros((1, span), jnp.float32), my_taps[:-1]], axis=0)
-    window = jnp.concatenate([earlier, my_taps], axis=1)
+    shifted = jnp.concatenate([jnp.zeros((1, span), jnp.float32), my_taps], axis=0)
+    window = jnp.concatenate([shifted[0:-1:2], shifted[1::2], shifted[2::2]], axis=1)
 
     lined = in_order.reshape(wide, span, width).transpose(0, 2, 1).reshape(wide * width, span)
     conv = causal_conv(window, lined, width)

time: 98.2 us -> 97.8 us (level)
  no operation moved by 1% of the time
where the time goes in v5:
time: 97.8 us; the launch traced here: 97.5 us
  waiting for transfers between devices  36.9 us (38%)
  starting transfers between devices  26.7 us (27%)
  blocking collectives  15.8 us (16%)
  Pallas kernels  8.46 us (9%)
  local copies, waits for them, and re-layouts  7.03 us (7%)
  other arithmetic  2.24 us (2%)
    all_to_all x1, starting transfers between devices, body(): incoming = lax.all_to_all(outgoing, 'ctx', 1, 0, tiled=True)  19.2 us
    all_to_all x1, waiting for transfers between devices, body(): incoming = lax.all_to_all(outgoing, 'ctx', 1, 0, tiled=True)  18.7 us
    all_to_all x1, waiting for transfers between devices, body(): conv = lax.all_to_all(conv, 'ctx', 0, 0, tiled=True)  18.2 us
    all_gather x1, blocking collectives, body(): total_sq = jnp.sum(lax.all_gather(squares, 'ch'), axis=0)  15.8 us
    pallas_call x1, Pallas kernels, causal_conv(): pl.pallas_call(lambda *refs: conv_kernel(width, *refs), out_shape=jax.Sha...  8.46 us
    all_to_all x1, starting transfers between devices, body(): conv = lax.all_to_all(conv, 'ctx', 0, 0, tiled=True)  7.49 us
    gather x1, local copies, waits for them, and re-layouts, body(): conv.reshape(wide, width, 2, rows).transpose(0, 2, 1, 3)  2.24 us
  transfers between devices with their start and end apart: 2, of which 2 were waited for; matrix products, arithmetic and copies ran while one was open for 1% of the time, Pallas kernels for 0%

profile of v5, /device:TPU:1, one launch (start us, length us, event | category | flops | bytes accessed | tf_op | source)
XLA Modules:
  0.0 97.5 jit_solution(17861297725537768860)
XLA Ops:
  0.0 1.1 %copy.56 = bf16[128,512]{0,1:T(8,128)(2,1)S(1)} copy(bf16[128,512]{1,0:T(8,128)(2,1)} %param.8) | data formatting | bytes 262144 | tf_op args[1]
  1.1 0.0 copy-done
  1.1 0.1 copy.57
  1.2 0.0 copy-done.3
  1.2 0.1 copy.58
  1.3 0.1 copy.59
  1.5 0.2 copy.60
  1.7 0.1 broadcast_in_dim.31
  1.8 0.1 convert_element_type.31
  2.0 0.7 maximum_bitcast_fusion
  2.8 19.2 %all-to-all-start = ((bf16[160,64,8]{0,2,1:T(8,128)(2,1)}), bf16[160,64,8]{0,2,1:T(8,128)(2,1)S(1)}, u32[]{:S(2)}, u32[]{:S(2)}) async-start(bf16[160,64,8]{0,2,1:T(8,128)(2,1)} %maximum_bitcast_fusion), calls=%async_computation | async-start | bytes 524288 | tf_op jit(solution)/shard_map/all_to_all | solution.py:94
  22.0 0.0 copy-done.2
  22.1 0.3 select_reduce_fusion
  22.5 18.7 %all-to-all-done = bf16[160,64,8]{0,2,1:T(8,128)(2,1)S(1)} async-done(((bf16[160,64,8]{0,2,1:T(8,128)(2,1)}), bf16[160,64,8]{0,2,1:T(8,128)(2,1)S(1)}, u32[]{:S(2)}, u32[]{:S(2)}) %all-to-all-start) | async-done | bytes 163872 | tf_op jit(solution)/shard_map/all_to_all | solution.py:94
  41.2 0.3 copy.61
  41.6 0.1 copy.62
  41.8 0.2 copy.63
  42.0 1.3 %gather_fusion = bf16[64,128,8]{1,2,0:T(8,128)(2,1)} fusion(bf16[64,128,8]{1,2,0:T(8,128)(2,1)S(1)} %copy.63, s32[1024]{0:T(1024)S(1)} %pad_clamp_fusion.1), kind=kCustom, calls=%fused_computation | custom fusion | bytes 262400 | tf_op jit(solution)/shard_map/gather | solution.py:96
  43.3 0.6 pad_maximum_fusion.1.refs_0_
  43.9 8.5 %shard_map.73 = f32[256,256]{1,0:T(8,128)} custom-call(f32[16,768]{1,0:T(8,128)} %pad_maximum_fusion.1.refs_0_, bf16[256,256]{1,0:T(8,128)(2,1)} %bitcast.49), custom_call_target="tpu_custom_call" | custom-call | flops 2147483648 | bytes 442368 | tf_op jit(solution)/shard_map/pallas_call | solution.py:61
  52.4 2.2 %gather_fusion.1 = f32[64,8,128]{2,1,0:T(8,128)} fusion(f32[64,8,128]{2,1,0:T(8,128)} %bitcast.53, s32[1024]{0:T(1024)S(1)} %pad_clamp_fusion), kind=kCustom, calls=%fused_computation.1 | custom fusion | bytes 524544 | tf_op jit(solution)/shard_map/gather | solution.py:106
  54.6 7.5 %all-to-all-start.1 = ((f32[64,8,128]{2,1,0:T(8,128)}), f32[64,8,128]{2,1,0:T(8,128)S(1)}, u32[]{:S(2)}, u32[]{:S(2)}) async-start(f32[64,8,128]{2,1,0:T(8,128)} %gather_fusion.1), calls=%async_computation.1 | async-start | bytes 524288 | tf_op jit(solution)/shard_map/all_to_all | solution.py:107
  62.1 0.0 copy-done.1
  62.1 0.1 copy.55
  62.2 0.0 copy-start.5
  62.2 18.2 %all-to-all-done.1 = f32[64,8,128]{2,1,0:T(8,128)S(1)} async-done(((f32[64,8,128]{2,1,0:T(8,128)}), f32[64,8,128]{2,1,0:T(8,128)S(1)}, u32[]{:S(2)}, u32[]{:S(2)}) %all-to-all-start.1) | async-done | bytes 262176 | tf_op jit(solution)/shard_map/all_to_all | solution.py:107
  80.5 0.0 copy-done.4
  80.5 0.2 multiply_reduce_fusion
  80.6 15.8 %all-gather.1 = f32[8,1,128]{2,1,0:T(1,128)S(1)} all-gather(f32[1,1,128]{2,1,0:T(1,128)S(1)} %bitcast.57), channel_id=2, replica_groups=mesh['ctx'=64,'ch'=8] {'ch'}, dimensions={0}, use_global_device_ids=true | all-gather | bytes 4608 | tf_op jit(solution)/shard_map/all_gather | solution.py:113
  96.5 0.0 copy-done.5
  96.5 0.2 multiply_convert_fusion
  96.7 0.8 copy.64
  (24 shorter events, 0.4 us)
Async XLA Ops:
  0.0 1.1 %copy-start = (bf16[128,512]{1,0:T(8,128)(2,1)S(1)}, bf16[128,512]{1,0:T(8,128)(2,1)}, u32[]{:S(2)}) copy-start(bf16[128,512]{1,0:T(8,128)(2,1)} %param.9) | copy-start | bytes 393220
  0.0 1.2 %copy-start.3 = (f32[128,32]{0,1:T(8,128)S(1)}, f32[128,32]{0,1:T(8,128)}, u32[]{:S(2)}) copy-start(f32[128,32]{0,1:T(8,128)} %param.10) | copy-start | bytes 49156
  2.8 19.3 %copy-start.2 = (s32[2080,3]{0,1:T(4,128)S(1)}, s32[2080,3]{0,1:T(4,128)}, u32[]{:S(2)}) copy-start(s32[2080,3]{0,1:T(4,128)} %param.13) | copy-start | bytes 74884
  2.8 38.5 %all-to-all-start = ((bf16[160,64,8]{0,2,1:T(8,128)(2,1)}), bf16[160,64,8]{0,2,1:T(8,128)(2,1)S(1)}, u32[]{:S(2)}, u32[]{:S(2)}) async-start(bf16[160,64,8]{0,2,1:T(8,128)(2,1)} %maximum_bitcast_fusion), calls=%async_computation | async-start | bytes 524288 | tf_op jit(solution)/shard_map/all_to_all | solution.py:94
  54.6 7.5 %copy-start.1 = (bf16[128,512]{1,0:T(8,128)(2,1)S(1)}, bf16[128,512]{1,0:T(8,128)(2,1)}, u32[]{:S(2)}) copy-start(bf16[128,512]{1,0:T(8,128)(2,1)} %param.7) | copy-start | bytes 393220
  54.6 25.9 %copy-start.4 = (f32[512]{0:T(512)S(1)}, f32[512]{0:T(512)}, u32[]{:S(2)}) copy-start(f32[512]{0:T(512)} %param.11) | copy-start | bytes 6148
  54.6 25.9 %all-to-all-start.1 = ((f32[64,8,128]{2,1,0:T(8,128)}), f32[64,8,128]{2,1,0:T(8,128)S(1)}, u32[]{:S(2)}, u32[]{:S(2)}) async-start(f32[64,8,128]{2,1,0:T(8,128)} %gather_fusion.1), calls=%async_computation.1 | async-start | bytes 524288 | tf_op jit(solution)/shard_map/all_to_all | solution.py:107
  62.2 34.2 %copy-start.5 = (f32[512]{0:T(512)S(1)}, f32[512]{0:T(512)}, u32[]{:S(2)}) copy-start(f32[512]{0:T(512)} %param.12) | copy-start | bytes 6148

commit v6 on v5

--- a/solution.py
+++ b/solution.py
@@ -23,10 +23,11 @@
     return lax.reduce_precision(values, exponent_bits=8, mantissa_bits=7)
 
 
-def conv_kernel(width, window_ref, signal_ref, out_ref, padded_ref):
-    rows = out_ref.shape[1]
-    lanes = out_ref.shape[0]
+def conv_kernel(width, device_ref, window_ref, signal_ref, out_ref, padded_ref):
+    rows = signal_ref.shape[1]
+    lanes = signal_ref.shape[0]
     pairs = window_ref.shape[0]
+    part = out_ref.shape[2]
     half = lanes // 2
     padded_ref[pl.ds(0, lanes), :] = jnp.zeros((lanes, rows), jnp.float32)
     padded_ref[pl.ds(lanes, lanes), :] = signal_ref[...].astype(jnp.float32)
@@ -49,19 +50,29 @@
         0, pairs // 2, lambda pair, acc: add_pair(acc, pair, 0, lanes),
         jnp.zeros((lanes, rows), jnp.float32),
     )
-    out_ref[pl.ds(0, half), :] = total[:half]
-    out_ref[pl.ds(half, half), :] = lax.fori_loop(
+    lower = lax.fori_loop(
         pairs // 2, pairs, lambda pair, acc: add_pair(acc, pair, half, half), total[half:],
     )
 
+    def place(values, first):
+        for row in range(values.shape[0] // width):
+            for piece in range(rows // part):
+                block = (first + row) * (rows // part) + piece
+                out_ref[device_ref[block]] = values[
+                    row * width : (row + 1) * width, piece * part : (piece + 1) * part
+                ]
 
-def causal_conv(window, signal, width):
+    place(total[:half], 0)
+    place(lower, half // width)
+
+
+def causal_conv(device_of, window, signal, width, part):
     lanes, rows = signal.shape
     blocks = 2 * window.shape[0]
     return pl.pallas_call(
         lambda *refs: conv_kernel(width, *refs),
-        out_shape=jax.ShapeDtypeStruct((lanes, rows), jnp.float32),
-        in_specs=[pl.BlockSpec(memory_space=pltpu.VMEM)] * 2,
+        out_shape=jax.ShapeDtypeStruct((lanes * rows // (width * part), width, part), jnp.float32),
+        in_specs=[pl.BlockSpec(memory_space=pltpu.SMEM)] + [pl.BlockSpec(memory_space=pltpu.VMEM)] * 2,
         out_specs=pl.BlockSpec(memory_space=pltpu.VMEM),
         scratch_shapes=[pltpu.VMEM((2 * lanes, rows), jnp.float32)],
         cost_estimate=pl.CostEstimate(
@@ -69,7 +80,7 @@
             bytes_accessed=window.size * 4 + signal.size * 2 + rows * lanes * 4,
             transcendentals=0,
         ),
-    )(window, signal)
+    )(device_of, window, signal)
 
 
 def body(query, key, value, filter_taps, conv_bias, norm_gain, pair_list):
@@ -102,8 +113,7 @@
     window = jnp.concatenate([shifted[0:-1:2], shifted[1::2], shifted[2::2]], axis=1)
 
     lined = in_order.reshape(wide, span, width).transpose(0, 2, 1).reshape(wide * width, span)
-    conv = causal_conv(window, lined, width)
-    conv = conv.reshape(wide, width, 2, rows).transpose(0, 2, 1, 3).reshape(blocks, width, rows)[holder]
+    conv = causal_conv(device_of, window, lined, width, rows)
     conv = lax.all_to_all(conv, "ctx", 0, 0, tiled=True)
     conv = conv.transpose(2, 0, 1).reshape(rows, channels)
 

time: 97.8 us -> 95.6 us (0.978)
  local copies, waits for them, and re-layouts: 7.03 us -> 4.79 us
    gather x1 -> x0, local copies, waits for them, and re-layouts: 2.24 us -> none  [body(): conv.reshape(wide, width, 2, rows).transpose(0, 2, 1, 3)]
  transfers between devices with their start and end apart: 2 -> 2, of which waited for: 2 -> 2; matrix products, arithmetic and copies ran while one was open for 1% -> 0% of each run, Pallas kernels for 0% -> 0%
where the time goes in v6:
time: 95.6 us; the launch traced here: 95.3 us
  waiting for transfers between devices  37.1 us (39%)
  starting transfers between devices  26.7 us (28%)
  blocking collectives  15.8 us (17%)
  Pallas kernels  8.48 us (9%)
  local copies, waits for them, and re-layouts  4.79 us (5%)
  other arithmetic  2.13 us (2%)
    all_to_all x1, starting transfers between devices, body(): incoming = lax.all_to_all(outgoing, 'ctx', 1, 0, tiled=True)  19.2 us
    all_to_all x1, waiting for transfers between devices, body(): incoming = lax.all_to_all(outgoing, 'ctx', 1, 0, tiled=True)  18.8 us
    all_to_all x1, waiting for transfers between devices, body(): conv = lax.all_to_all(conv, 'ctx', 0, 0, tiled=True)  18.2 us
    all_gather x1, blocking collectives, body(): total_sq = jnp.sum(lax.all_gather(squares, 'ch'), axis=0)  15.8 us
    pallas_call x1, Pallas kernels, causal_conv(): pl.pallas_call(lambda *refs: conv_kernel(width, *refs), out_shape=jax.Sha...  8.48 us
    all_to_all x1, starting transfers between devices, body(): conv = lax.all_to_all(conv, 'ctx', 0, 0, tiled=True)  7.48 us
  transfers between devices with their start and end apart: 2, of which 2 were waited for; matrix products, arithmetic and copies ran while one was open for 0% of the time, Pallas kernels for 0%

profile of v6, /device:TPU:1, one launch (start us, length us, event | category | flops | bytes accessed | tf_op | source)
XLA Modules:
  0.0 95.3 jit_solution(11792405561962708164)
XLA Ops:
  0.0 1.1 %copy.57 = bf16[128,512]{0,1:T(8,128)(2,1)S(1)} copy(bf16[128,512]{1,0:T(8,128)(2,1)} %param.8) | data formatting | bytes 262144 | tf_op args[1]
  1.1 0.0 copy-done
  1.1 0.1 copy.58
  1.2 0.0 copy-done.3
  1.2 0.1 copy.59
  1.3 0.1 copy.60
  1.5 0.2 copy.61
  1.7 0.1 broadcast_in_dim.27
  1.8 0.1 convert_element_type.31
  2.0 0.7 maximum_bitcast_fusion
  2.8 19.2 %all-to-all-start = ((bf16[160,64,8]{0,2,1:T(8,128)(2,1)}), bf16[160,64,8]{0,2,1:T(8,128)(2,1)S(1)}, u32[]{:S(2)}, u32[]{:S(2)}) async-start(bf16[160,64,8]{0,2,1:T(8,128)(2,1)} %maximum_bitcast_fusion), calls=%async_computation | async-start | bytes 524288 | tf_op jit(solution)/shard_map/all_to_all | solution.py:105
  22.0 0.0 copy-done.2
  22.1 0.2 select_reduce_fusion.refs_0_
  22.4 18.8 %all-to-all-done = bf16[160,64,8]{0,2,1:T(8,128)(2,1)S(1)} async-done(((bf16[160,64,8]{0,2,1:T(8,128)(2,1)}), bf16[160,64,8]{0,2,1:T(8,128)(2,1)S(1)}, u32[]{:S(2)}, u32[]{:S(2)}) %all-to-all-start) | async-done | bytes 163872 | tf_op jit(solution)/shard_map/all_to_all | solution.py:105
  41.2 0.3 copy.62
  41.5 0.0 copy-done.6
  41.6 0.1 copy.63
  41.8 0.2 copy.64
  42.0 1.3 %gather_fusion = bf16[64,128,8]{1,2,0:T(8,128)(2,1)} fusion(bf16[64,128,8]{1,2,0:T(8,128)(2,1)S(1)} %copy.64, s32[1024]{0:T(1024)S(1)} %pad_clamp_fusion), kind=kCustom, calls=%fused_computation | custom fusion | bytes 262400 | tf_op jit(solution)/shard_map/gather | solution.py:107
  43.3 0.6 pad_maximum_fusion.1.refs_1_
  43.9 8.5 %shard_map.73 = f32[64,8,128]{2,1,0:T(8,128)} custom-call(s32[64]{0:T(128)} %copy-done.6, f32[16,768]{1,0:T(8,128)} %pad_maximum_fusion.1.refs_1_, bf16[256,256]{1,0:T(8,128)(2,1)} %bitcast.40), custom_call_target="tpu_custom_call" | custom-call | flops 2147483648 | bytes 442368 | tf_op jit(solution)/shard_map/pallas_call | solution.py:72
  52.4 7.5 %all-to-all-start.1 = ((f32[64,8,128]{2,1,0:T(8,128)}), f32[64,8,128]{2,1,0:T(8,128)S(1)}, u32[]{:S(2)}, u32[]{:S(2)}) async-start(f32[64,8,128]{2,1,0:T(8,128)} %shard_map.73), calls=%async_computation.1 | async-start | bytes 524288 | tf_op jit(solution)/shard_map/all_to_all | solution.py:117
  59.9 0.0 copy-done.1
  59.9 0.1 copy.56
  60.0 0.0 copy-start.5
  60.0 18.2 %all-to-all-done.1 = f32[64,8,128]{2,1,0:T(8,128)S(1)} async-done(((f32[64,8,128]{2,1,0:T(8,128)}), f32[64,8,128]{2,1,0:T(8,128)S(1)}, u32[]{:S(2)}, u32[]{:S(2)}) %all-to-all-start.1) | async-done | bytes 262176 | tf_op jit(solution)/shard_map/all_to_all | solution.py:117
  78.2 0.0 copy-done.4
  78.2 0.2 multiply_reduce_fusion
  78.4 15.8 %all-gather.1 = f32[8,1,128]{2,1,0:T(1,128)S(1)} all-gather(f32[1,1,128]{2,1,0:T(1,128)S(1)} %bitcast.47), channel_id=2, replica_groups=mesh['ctx'=64,'ch'=8] {'ch'}, dimensions={0}, use_global_device_ids=true | all-gather | bytes 4608 | tf_op jit(solution)/shard_map/all_gather | solution.py:123
  94.3 0.0 copy-done.5
  94.3 0.2 multiply_convert_fusion
  94.5 0.8 copy.65
  (24 shorter events, 0.3 us)
Async XLA Ops:
  0.0 1.1 %copy-start = (bf16[128,512]{1,0:T(8,128)(2,1)S(1)}, bf16[128,512]{1,0:T(8,128)(2,1)}, u32[]{:S(2)}) copy-start(bf16[128,512]{1,0:T(8,128)(2,1)} %param.9) | copy-start | bytes 393220
  0.0 1.2 %copy-start.3 = (f32[128,32]{0,1:T(8,128)S(1)}, f32[128,32]{0,1:T(8,128)}, u32[]{:S(2)}) copy-start(f32[128,32]{0,1:T(8,128)} %param.10) | copy-start | bytes 49156
  2.8 19.3 %copy-start.2 = (s32[2080,3]{0,1:T(4,128)S(1)}, s32[2080,3]{0,1:T(4,128)}, u32[]{:S(2)}) copy-start(s32[2080,3]{0,1:T(4,128)} %param.13) | copy-start | bytes 74884
  2.8 38.5 %all-to-all-start = ((bf16[160,64,8]{0,2,1:T(8,128)(2,1)}), bf16[160,64,8]{0,2,1:T(8,128)(2,1)S(1)}, u32[]{:S(2)}, u32[]{:S(2)}) async-start(bf16[160,64,8]{0,2,1:T(8,128)(2,1)} %maximum_bitcast_fusion), calls=%async_computation | async-start | bytes 524288 | tf_op jit(solution)/shard_map/all_to_all | solution.py:105
  22.4 19.2 %copy-start.6 = (s32[64]{0:T(128)}, s32[64]{0:T(128)S(1)}, u32[]{:S(2)}) copy-start(s32[64]{0:T(128)S(1)} %select_reduce_fusion.refs_0_) | copy-start | bytes 772
  52.4 7.5 %copy-start.1 = (bf16[128,512]{1,0:T(8,128)(2,1)S(1)}, bf16[128,512]{1,0:T(8,128)(2,1)}, u32[]{:S(2)}) copy-start(bf16[128,512]{1,0:T(8,128)(2,1)} %param.7) | copy-start | bytes 393220
  52.4 25.9 %copy-start.4 = (f32[512]{0:T(512)S(1)}, f32[512]{0:T(512)}, u32[]{:S(2)}) copy-start(f32[512]{0:T(512)} %param.11) | copy-start | bytes 6148
  52.4 25.9 %all-to-all-start.1 = ((f32[64,8,128]{2,1,0:T(8,128)}), f32[64,8,128]{2,1,0:T(8,128)S(1)}, u32[]{:S(2)}, u32[]{:S(2)}) async-start(f32[64,8,128]{2,1,0:T(8,128)} %shard_map.73), calls=%async_computation.1 | async-start | bytes 524288 | tf_op jit(solution)/shard_map/all_to_all | solution.py:117
  60.0 34.3 %copy-start.5 = (f32[512]{0:T(512)S(1)}, f32[512]{0:T(512)}, u32[]{:S(2)}) copy-start(f32[512]{0:T(512)} %param.12) | copy-start | bytes 6148

commit v7 on v6

--- a/solution.py
+++ b/solution.py
@@ -23,14 +23,19 @@
     return lax.reduce_precision(values, exponent_bits=8, mantissa_bits=7)
 
 
-def conv_kernel(width, device_ref, window_ref, signal_ref, out_ref, padded_ref):
-    rows = signal_ref.shape[1]
-    lanes = signal_ref.shape[0]
+def conv_kernel(width, device_ref, window_ref, incoming_ref, out_ref, padded_ref):
+    rows = window_ref.shape[1] // 3
     pairs = window_ref.shape[0]
     part = out_ref.shape[2]
+    lanes = 2 * pairs * width
     half = lanes // 2
     padded_ref[pl.ds(0, lanes), :] = jnp.zeros((lanes, rows), jnp.float32)
-    padded_ref[pl.ds(lanes, lanes), :] = signal_ref[...].astype(jnp.float32)
+    for block in range(incoming_ref.shape[0]):
+        line = lanes + (block // (rows // part)) * width
+        column = (block % (rows // part)) * part
+        padded_ref[pl.ds(line, width), pl.ds(column, part)] = incoming_ref[
+            device_ref[block], pl.ds(0, width), :
+        ].astype(jnp.float32)
 
     def add_lag(total, block, lag, offset, count):
         block_hi = block.astype(jnp.bfloat16)
@@ -66,21 +71,22 @@
     place(lower, half // width)
 
 
-def causal_conv(device_of, window, signal, width, part):
-    lanes, rows = signal.shape
-    blocks = 2 * window.shape[0]
+def causal_conv(device_of, window, incoming, width):
+    blocks, _, part = incoming.shape
+    rows = window.shape[1] // 3
+    lanes = blocks * part // rows * width
     return pl.pallas_call(
         lambda *refs: conv_kernel(width, *refs),
-        out_shape=jax.ShapeDtypeStruct((lanes * rows // (width * part), width, part), jnp.float32),
+        out_shape=jax.ShapeDtypeStruct((blocks, width, part), jnp.float32),
         in_specs=[pl.BlockSpec(memory_space=pltpu.SMEM)] + [pl.BlockSpec(memory_space=pltpu.VMEM)] * 2,
         out_specs=pl.BlockSpec(memory_space=pltpu.VMEM),
         scratch_shapes=[pltpu.VMEM((2 * lanes, rows), jnp.float32)],
         cost_estimate=pl.CostEstimate(
-            flops=4 * rows * rows * lanes * blocks,
-            bytes_accessed=window.size * 4 + signal.size * 2 + rows * lanes * 4,
+            flops=4 * rows * rows * lanes * 2 * window.shape[0],
+            bytes_accessed=window.size * 4 + incoming.size * 2 + rows * lanes * 4,
             transcendentals=0,
         ),
-    )(device_of, window, signal)
+    )(device_of, window, incoming)
 
 
 def body(query, key, value, filter_taps, conv_bias, norm_gain, pair_list):
@@ -97,23 +103,25 @@
 
     taps_hi = to_bf16_grid(filter_taps)
     taps_lo = filter_taps - taps_hi
-    coded = jnp.stack([taps_hi.T, taps_lo.T], axis=1).reshape(groups, 2, rows // width, width)
-    coded = jnp.repeat(coded, share, axis=0).reshape(blocks, 2 * rows // width, width)
-    coded = coded.transpose(1, 0, 2).reshape(2 * rows // width, channels)
-    outgoing = jnp.concatenate([signal, coded.astype(jnp.bfloat16)], axis=0)
-
-    incoming = lax.all_to_all(outgoing, "ctx", 1, 0, tiled=True)
-    incoming = incoming.reshape(blocks, rows + 2 * rows // width, width)
-    in_order = incoming[:, :rows, :][device_of]
-    taps_in = incoming[:, rows:, :].astype(jnp.float32).reshape(blocks, 2, rows)
+    coded = jnp.repeat(jnp.stack([taps_hi.T, taps_lo.T], axis=1), share, axis=0)
+    tile = 16
+    outgoing = jnp.concatenate(
+        [
+            signal.T.reshape(blocks, width, rows),
+            coded.astype(jnp.bfloat16),
+            jnp.zeros((blocks, tile - width - 2, rows), jnp.bfloat16),
+        ],
+        axis=1,
+    )
+    incoming = lax.all_to_all(outgoing, "ctx", 0, 0, tiled=True)
+    taps_in = incoming[:, width : width + 2, :].astype(jnp.float32)
     span = 2 * rows
     wide = blocks // 2
     my_taps = (taps_in[:, 0, :] + taps_in[:, 1, :]).reshape(wide, span)
     shifted = jnp.concatenate([jnp.zeros((1, span), jnp.float32), my_taps], axis=0)
     window = jnp.concatenate([shifted[0:-1:2], shifted[1::2], shifted[2::2]], axis=1)
 
-    lined = in_order.reshape(wide, span, width).transpose(0, 2, 1).reshape(wide * width, span)
-    conv = causal_conv(device_of, window, lined, width, rows)
+    conv = causal_conv(device_of, window, incoming, width)
     conv = lax.all_to_all(conv, "ctx", 0, 0, tiled=True)
     conv = conv.transpose(2, 0, 1).reshape(rows, channels)
 

time: 95.6 us -> 94.6 us (0.990)
  blocking collectives: 15.8 us -> 41.5 us
  waiting for transfers between devices: 37.1 us -> 18.3 us
  starting transfers between devices: 26.7 us -> 19.2 us
  local copies, waits for them, and re-layouts: 4.79 us -> 1.37 us
  other arithmetic: 2.13 us -> 5.11 us
    all_to_all x0 -> x1, blocking collectives: none -> 25.7 us  [body(): conv = lax.all_to_all(conv, 'ctx', 0, 0, tiled=True)]
    all_to_all x2 -> x1, waiting for transfers between devices: 37.1 us -> 18.3 us  [body(): incoming = lax.all_to_all(outgoing, 'ctx', 0, 0, tiled=True)]
    all_to_all x2 -> x1, starting transfers between devices: 26.7 us -> 19.2 us  [body(): incoming = lax.all_to_all(outgoing, 'ctx', 0, 0, tiled=True)]
    gather x1 -> x0, local copies, waits for them, and re-layouts: 1.27 us -> none  [body(): in_order = incoming[:, :rows, :][device_of]]
    transpose x1, other arithmetic: 0.01 us -> 1 us  [body(): signal.T.reshape(blocks, width, rows)]
  transfers between devices with their start and end apart: 2 -> 1, of which waited for: 2 -> 1; matrix products, arithmetic and copies ran while one was open for 0% -> 1% of each run, Pallas kernels for 0% -> 0%
where the time goes in v7:
time: 94.6 us; the launch traced here: 94.2 us
  blocking collectives  41.5 us (44%)
  starting transfers between devices  19.2 us (20%)
  waiting for transfers between devices  18.3 us (19%)
  Pallas kernels  8.56 us (9%)
  other arithmetic  5.11 us (5%)
  local copies, waits for them, and re-layouts  1.37 us (1%)
    all_to_all x1, blocking collectives, body(): conv = lax.all_to_all(conv, 'ctx', 0, 0, tiled=True)  25.7 us
    all_to_all x1, starting transfers between devices, body(): incoming = lax.all_to_all(outgoing, 'ctx', 0, 0, tiled=True)  19.2 us
    all_to_all x1, waiting for transfers between devices, body(): incoming = lax.all_to_all(outgoing, 'ctx', 0, 0, tiled=True)  18.3 us
    all_gather x1, blocking collectives, body(): total_sq = jnp.sum(lax.all_gather(squares, 'ch'), axis=0)  15.8 us
    pallas_call x1, Pallas kernels, causal_conv(): pl.pallas_call(lambda *refs: conv_kernel(width, *refs), out_shape=jax.Sha...  8.56 us
  transfers between devices with their start and end apart: 1, of which 1 were waited for; matrix products, arithmetic and copies ran while one was open for 1% of the time, Pallas kernels for 0%

profile of v7, /device:TPU:1, one launch (start us, length us, event | category | flops | bytes accessed | tf_op | source)
XLA Modules:
  0.0 94.2 jit_solution(14172667830435745421)
XLA Ops:
  0.0 0.7 fusion.6
  0.7 1.0 %fusion.2 = bf16[512,128]{0,1:T(8,128)(2,1)S(1)} fusion(bf16[128,512]{1,0:T(8,128)(2,1)} %param.9, bf16[128,512]{1,0:T(8,128)(2,1)} %param.8), kind=kLoop, calls=%fused_computation.9 | loop fusion | flops 327680 | bytes 393216 | tf_op jit(solution)/shard_map/transpose | solution.py:110
  1.8 0.1 copy.14
  1.9 0.1 pad.6.clone
  2.0 0.8 maximum_maximum_fusion
  2.8 0.0 copy-start.4
  2.8 19.2 %all-to-all-start = ((bf16[64,16,128]{2,1,0:T(8,128)(2,1)}), bf16[64,16,128]{2,1,0:T(8,128)(2,1)S(1)}, u32[]{:S(2)}, u32[]{:S(2)}) async-start(bf16[64,16,128]{2,1,0:T(8,128)(2,1)} %maximum_maximum_fusion), calls=%async_computation | async-start | bytes 524288 | tf_op jit(solution)/shard_map/all_to_all | solution.py:116
  22.1 0.0 copy-done.4
  22.2 0.8 select_reduce_fusion.refs_0_
  23.0 18.3 %all-to-all-done.refs_2_ = bf16[64,16,128]{2,1,0:T(8,128)(2,1)S(1)} async-done(((bf16[64,16,128]{2,1,0:T(8,128)(2,1)}), bf16[64,16,128]{2,1,0:T(8,128)(2,1)S(1)}, u32[]{:S(2)}, u32[]{:S(2)}) %all-to-all-start) | async-done | bytes 262176 | tf_op jit(solution)/shard_map/all_to_all | solution.py:116
  41.3 0.0 copy-start.3
  41.3 0.1 fusion.3
  41.5 0.6 pad_maximum_fusion.refs_1_
  42.1 0.0 copy-done.3
  42.1 8.6 %shard_map.73 = f32[64,8,128]{2,1,0:T(8,128)} custom-call(s32[64]{0:T(128)} %select_reduce_fusion.refs_0_, f32[16,768]{1,0:T(8,128)} %pad_maximum_fusion.refs_1_, bf16[64,16,128]{2,1,0:T(8,128)(2,1)} %copy-done.3), custom_call_target="tpu_custom_call" | custom-call | flops 2147483648 | bytes 573440 | tf_op jit(solution)/shard_map/pallas_call | solution.py:78
  50.7 25.7 %all_to_all.10 = f32[64,8,128]{2,1,0:T(8,128)S(1)} all-to-all(f32[64,8,128]{2,1,0:T(8,128)} %shard_map.73), channel_id=1, replica_groups=mesh['ctx'=64,'ch'=8] {'ctx'}, dimensions={0} | all-to-all | bytes 524288 | tf_op jit(solution)/shard_map/all_to_all | solution.py:125
  76.4 0.0 copy-start
  76.4 0.0 copy-start.1
  76.4 0.0 copy-start.2
  76.4 0.0 copy-start.5
  76.4 0.1 copy.16
  76.5 0.8 copy-done
  77.3 0.1 copy-done.1
  77.4 0.1 copy-done.2
  77.4 0.0 copy-done.5
  77.4 0.0 copy-start.6
  77.4 0.2 multiply_reduce_fusion
  77.6 15.8 %all-gather.1 = f32[8,1,128]{2,1,0:T(1,128)S(1)} all-gather(f32[1,1,128]{2,1,0:T(1,128)S(1)} %bitcast.19), channel_id=2, replica_groups=mesh['ctx'=64,'ch'=8] {'ch'}, dimensions={0}, use_global_device_ids=true | all-gather | bytes 4608 | tf_op jit(solution)/shard_map/all_gather | solution.py:131
  93.5 0.0 copy-done.6
  93.5 0.8 multiply_convert_fusion
  (14 shorter events, 0.3 us)
Async XLA Ops:
  2.8 19.3 %copy-start.4 = (s32[2080,3]{0,1:T(4,128)S(1)}, s32[2080,3]{0,1:T(4,128)}, u32[]{:S(2)}) copy-start(s32[2080,3]{0,1:T(4,128)} %param.13) | copy-start | bytes 74884
  2.8 38.5 %all-to-all-start = ((bf16[64,16,128]{2,1,0:T(8,128)(2,1)}), bf16[64,16,128]{2,1,0:T(8,128)(2,1)S(1)}, u32[]{:S(2)}, u32[]{:S(2)}) async-start(bf16[64,16,128]{2,1,0:T(8,128)(2,1)} %maximum_maximum_fusion), calls=%async_computation | async-start | bytes 524288 | tf_op jit(solution)/shard_map/all_to_all | solution.py:116
  41.3 0.8 copy-start.3
  76.4 0.9 copy-start
  76.4 1.0 %copy-start.1 = (bf16[128,512]{1,0:T(8,128)(2,1)S(1)}, bf16[128,512]{1,0:T(8,128)(2,1)}, u32[]{:S(2)}) copy-start(bf16[128,512]{1,0:T(8,128)(2,1)} %param.8) | copy-start | bytes 393220
  76.4 1.0 %copy-start.2 = (bf16[128,512]{1,0:T(8,128)(2,1)S(1)}, bf16[128,512]{1,0:T(8,128)(2,1)}, u32[]{:S(2)}) copy-start(bf16[128,512]{1,0:T(8,128)(2,1)} %param.7) | copy-start | bytes 393220
  76.4 1.0 %copy-start.5 = (f32[512]{0:T(512)S(1)}, f32[512]{0:T(512)}, u32[]{:S(2)}) copy-start(f32[512]{0:T(512)} %param.11) | copy-start | bytes 6148
  77.4 16.0 %copy-start.6 = (f32[512]{0:T(512)S(1)}, f32[512]{0:T(512)}, u32[]{:S(2)}) copy-start(f32[512]{0:T(512)} %param.12) | copy-start | bytes 6148

commit v8 on v7

--- a/solution.py
+++ b/solution.py
@@ -23,7 +23,7 @@
     return lax.reduce_precision(values, exponent_bits=8, mantissa_bits=7)
 
 
-def conv_kernel(width, device_ref, window_ref, incoming_ref, out_ref, padded_ref):
+def conv_kernel(width, device_ref, window_ref, window_lo_ref, incoming_ref, out_ref, padded_ref):
     rows = window_ref.shape[1] // 3
     pairs = window_ref.shape[0]
     part = out_ref.shape[2]
@@ -37,19 +37,26 @@
             device_ref[block], pl.ds(0, width), :
         ].astype(jnp.float32)
 
-    def add_lag(total, block, lag, offset, count):
-        block_hi = block.astype(jnp.bfloat16)
-        block_lo = (block - block_hi.astype(jnp.float32)).astype(jnp.bfloat16)
+    def add_lag(total, block_hi, block_lo, lag, offset, count):
         start = pl.multiple_of(lanes - lag * width + offset, width)
         moved = padded_ref[pl.ds(start, count), :].astype(jnp.bfloat16)
         total = total + jnp.dot(moved, block_hi, preferred_element_type=jnp.float32)
         return total + jnp.dot(moved, block_lo, preferred_element_type=jnp.float32)
 
+    def skew(ref, pair):
+        window = jnp.broadcast_to(ref[pl.ds(pair, 1), :], (rows, 3 * rows))
+        return pltpu.roll(window, 2 * rows, 1, stride=1, stride_axis=0)
+
     def add_pair(total, pair, offset, count):
-        window = jnp.broadcast_to(window_ref[pl.ds(pair, 1), :], (rows, 3 * rows))
-        skewed = pltpu.roll(window, 2 * rows, 1, stride=1, stride_axis=0)
-        total = add_lag(total, skewed[:, :rows], 2 * pair, offset, count)
-        return add_lag(total, skewed[:, rows : 2 * rows], 2 * pair + 1, offset, count)
+        high = skew(window_ref, pair)
+        low = skew(window_lo_ref, pair)
+        first = (high[:, :rows].astype(jnp.bfloat16), low[:, :rows].astype(jnp.bfloat16))
+        total = add_lag(total, *first, 2 * pair, offset, count)
+        second = (
+            high[:, rows : 2 * rows].astype(jnp.bfloat16),
+            low[:, rows : 2 * rows].astype(jnp.bfloat16),
+        )
+        return add_lag(total, *second, 2 * pair + 1, offset, count)
 
     total = lax.fori_loop(
         0, pairs // 2, lambda pair, acc: add_pair(acc, pair, 0, lanes),
@@ -72,13 +79,15 @@
 
 
 def causal_conv(device_of, window, incoming, width):
+    window_hi = to_bf16_grid(window)
+    window_lo = to_bf16_grid(window - window_hi)
     blocks, _, part = incoming.shape
     rows = window.shape[1] // 3
     lanes = blocks * part // rows * width
     return pl.pallas_call(
         lambda *refs: conv_kernel(width, *refs),
         out_shape=jax.ShapeDtypeStruct((blocks, width, part), jnp.float32),
-        in_specs=[pl.BlockSpec(memory_space=pltpu.SMEM)] + [pl.BlockSpec(memory_space=pltpu.VMEM)] * 2,
+        in_specs=[pl.BlockSpec(memory_space=pltpu.SMEM)] + [pl.BlockSpec(memory_space=pltpu.VMEM)] * 3,
         out_specs=pl.BlockSpec(memory_space=pltpu.VMEM),
         scratch_shapes=[pltpu.VMEM((2 * lanes, rows), jnp.float32)],
         cost_estimate=pl.CostEstimate(
@@ -86,7 +95,7 @@
             bytes_accessed=window.size * 4 + incoming.size * 2 + rows * lanes * 4,
             transcendentals=0,
         ),
-    )(device_of, window, incoming)
+    )(device_of, window_hi, window_lo, incoming)
 
 
 def body(query, key, value, filter_taps, conv_bias, norm_gain, pair_list):

time: 94.6 us -> 94.3 us (level)
  no operation moved by 1% of the time
where the time goes in v8:
time: 94.3 us; the launch traced here: 93.9 us
  blocking collectives  41.5 us (44%)
  starting transfers between devices  19.2 us (20%)
  waiting for transfers between devices  18.3 us (19%)
  Pallas kernels  8.18 us (9%)
  other arithmetic  5.1 us (5%)
  local copies, waits for them, and re-layouts  1.37 us (1%)
    all_to_all x1, blocking collectives, body(): conv = lax.all_to_all(conv, 'ctx', 0, 0, tiled=True)  25.7 us
    all_to_all x1, starting transfers between devices, body(): incoming = lax.all_to_all(outgoing, 'ctx', 0, 0, tiled=True)  19.2 us
    all_to_all x1, waiting for transfers between devices, body(): incoming = lax.all_to_all(outgoing, 'ctx', 0, 0, tiled=True)  18.3 us
    all_gather x1, blocking collectives, body(): total_sq = jnp.sum(lax.all_gather(squares, 'ch'), axis=0)  15.8 us
    pallas_call x1, Pallas kernels, causal_conv(): pl.pallas_call(lambda *refs: conv_kernel(width, *refs), out_shape=jax.Sha...  8.18 us
  transfers between devices with their start and end apart: 1, of which 1 were waited for; matrix products, arithmetic and copies ran while one was open for 1% of the time, Pallas kernels for 0%

profile of v8, /device:TPU:1, one launch (start us, length us, event | category | flops | bytes accessed | tf_op | source)
XLA Modules:
  0.0 93.9 jit_solution(389596290172366955)
XLA Ops:
  0.0 0.7 fusion.7
  0.7 1.0 %fusion.2 = bf16[512,128]{0,1:T(8,128)(2,1)S(1)} fusion(bf16[128,512]{1,0:T(8,128)(2,1)} %param.9, bf16[128,512]{1,0:T(8,128)(2,1)} %param.8), kind=kLoop, calls=%fused_computation.9 | loop fusion | flops 327680 | bytes 393216 | tf_op jit(solution)/shard_map/transpose | solution.py:119
  1.8 0.1 copy.14
  1.9 0.1 pad.6.clone
  2.0 0.8 maximum_maximum_fusion
  2.8 0.0 copy-start.4
  2.8 19.2 %all-to-all-start = ((bf16[64,16,128]{2,1,0:T(8,128)(2,1)}), bf16[64,16,128]{2,1,0:T(8,128)(2,1)S(1)}, u32[]{:S(2)}, u32[]{:S(2)}) async-start(bf16[64,16,128]{2,1,0:T(8,128)(2,1)} %maximum_maximum_fusion), calls=%async_computation | async-start | bytes 524288 | tf_op jit(solution)/shard_map/all_to_all | solution.py:125
  22.1 0.0 copy-done.4
  22.2 0.8 select_reduce_fusion.refs_0_
  22.9 18.3 %all-to-all-done.refs_3_ = bf16[64,16,128]{2,1,0:T(8,128)(2,1)S(1)} async-done(((bf16[64,16,128]{2,1,0:T(8,128)(2,1)}), bf16[64,16,128]{2,1,0:T(8,128)(2,1)S(1)}, u32[]{:S(2)}, u32[]{:S(2)}) %all-to-all-start) | async-done | bytes 262176 | tf_op jit(solution)/shard_map/all_to_all | solution.py:125
  41.3 0.0 copy-start.3
  41.3 0.1 fusion.4
  41.5 0.7 subtract_reduce-precision_fusion
  42.1 0.0 copy-done.3
  42.1 8.2 %shard_map.73 = f32[64,8,128]{2,1,0:T(8,128)} custom-call(s32[64]{0:T(128)} %select_reduce_fusion.refs_0_, f32[16,768]{1,0:T(8,128)} %get-tuple-element.8.refs_1_, f32[16,768]{1,0:T(8,128)} %get-tuple-element.7.refs_2_, bf16[64,16,128]{2,1,0:T(8,128)(2,1)} %copy-done.3), custom_call_target="tpu_custom_call" | custom-call | flops 2147483648 | bytes 573440 | tf_op jit(solution)/shard_map/pallas_call | solution.py:87
  50.3 25.7 %all_to_all.10 = f32[64,8,128]{2,1,0:T(8,128)S(1)} all-to-all(f32[64,8,128]{2,1,0:T(8,128)} %shard_map.73), channel_id=1, replica_groups=mesh['ctx'=64,'ch'=8] {'ctx'}, dimensions={0} | all-to-all | bytes 524288 | tf_op jit(solution)/shard_map/all_to_all | solution.py:134
  76.0 0.0 copy-start
  76.0 0.0 copy-start.1
  76.0 0.0 copy-start.2
  76.0 0.0 copy-start.5
  76.1 0.1 copy.16
  76.2 0.8 copy-done
  76.9 0.1 copy-done.1
  77.0 0.1 copy-done.2
  77.1 0.0 copy-done.5
  77.1 0.0 copy-start.6
  77.1 0.2 multiply_reduce_fusion
  77.2 15.8 %all-gather.1 = f32[8,1,128]{2,1,0:T(1,128)S(1)} all-gather(f32[1,1,128]{2,1,0:T(1,128)S(1)} %bitcast.19), channel_id=2, replica_groups=mesh['ctx'=64,'ch'=8] {'ch'}, dimensions={0}, use_global_device_ids=true | all-gather | bytes 4608 | tf_op jit(solution)/shard_map/all_gather | solution.py:140
  93.1 0.0 copy-done.6
  93.1 0.8 multiply_convert_fusion
  (14 shorter events, 0.3 us)
Async XLA Ops:
  2.8 19.3 %copy-start.4 = (s32[2080,3]{0,1:T(4,128)S(1)}, s32[2080,3]{0,1:T(4,128)}, u32[]{:S(2)}) copy-start(s32[2080,3]{0,1:T(4,128)} %param.13) | copy-start | bytes 74884
  2.8 38.5 %all-to-all-start = ((bf16[64,16,128]{2,1,0:T(8,128)(2,1)}), bf16[64,16,128]{2,1,0:T(8,128)(2,1)S(1)}, u32[]{:S(2)}, u32[]{:S(2)}) async-start(bf16[64,16,128]{2,1,0:T(8,128)(2,1)} %maximum_maximum_fusion), calls=%async_computation | async-start | bytes 524288 | tf_op jit(solution)/shard_map/all_to_all | solution.py:125
  41.3 0.9 copy-start.3
  76.0 0.9 copy-start
  76.0 1.0 %copy-start.1 = (bf16[128,512]{1,0:T(8,128)(2,1)S(1)}, bf16[128,512]{1,0:T(8,128)(2,1)}, u32[]{:S(2)}) copy-start(bf16[128,512]{1,0:T(8,128)(2,1)} %param.8) | copy-start | bytes 393220
  76.0 1.0 %copy-start.2 = (bf16[128,512]{1,0:T(8,128)(2,1)S(1)}, bf16[128,512]{1,0:T(8,128)(2,1)}, u32[]{:S(2)}) copy-start(bf16[128,512]{1,0:T(8,128)(2,1)} %param.7) | copy-start | bytes 393220
  76.0 1.0 %copy-start.5 = (f32[512]{0:T(512)S(1)}, f32[512]{0:T(512)}, u32[]{:S(2)}) copy-start(f32[512]{0:T(512)} %param.11) | copy-start | bytes 6148
  77.1 16.0 %copy-start.6 = (f32[512]{0:T(512)S(1)}, f32[512]{0:T(512)}, u32[]{:S(2)}) copy-start(f32[512]{0:T(512)} %param.12) | copy-start | bytes 6148

commit v9 on v8

--- a/solution.py
+++ b/solution.py
@@ -58,14 +58,6 @@
         )
         return add_lag(total, *second, 2 * pair + 1, offset, count)
 
-    total = lax.fori_loop(
-        0, pairs // 2, lambda pair, acc: add_pair(acc, pair, 0, lanes),
-        jnp.zeros((lanes, rows), jnp.float32),
-    )
-    lower = lax.fori_loop(
-        pairs // 2, pairs, lambda pair, acc: add_pair(acc, pair, half, half), total[half:],
-    )
-
     def place(values, first):
         for row in range(values.shape[0] // width):
             for piece in range(rows // part):
@@ -74,8 +66,19 @@
                     row * width : (row + 1) * width, piece * part : (piece + 1) * part
                 ]
 
-    place(total[:half], 0)
-    place(lower, half // width)
+    quarters = 4
+    quarter = lanes // quarters
+    total = jnp.zeros((lanes, rows), jnp.float32)
+    for index in range(quarters):
+        first = index * quarter
+        total = lax.fori_loop(
+            index * pairs // quarters,
+            (index + 1) * pairs // quarters,
+            lambda pair, acc, first=first: add_pair(acc, pair, first, lanes - first),
+            total,
+        )
+        place(total[:quarter], first // width)
+        total = total[quarter:]
 
 
 def causal_conv(device_of, window, incoming, width):

time: 94.3 us -> 94 us (level)
  no operation moved by 1% of the time
where the time goes in v9:
time: 94 us; the launch traced here: 93.6 us
  blocking collectives  41.5 us (44%)
  starting transfers between devices  19.2 us (20%)
  waiting for transfers between devices  18.3 us (19%)
  Pallas kernels  7.93 us (8%)
  other arithmetic  5.1 us (5%)
  local copies, waits for them, and re-layouts  1.37 us (1%)
    all_to_all x1, blocking collectives, body(): conv = lax.all_to_all(conv, 'ctx', 0, 0, tiled=True)  25.7 us
    all_to_all x1, starting transfers between devices, body(): incoming = lax.all_to_all(outgoing, 'ctx', 0, 0, tiled=True)  19.2 us
    all_to_all x1, waiting for transfers between devices, body(): incoming = lax.all_to_all(outgoing, 'ctx', 0, 0, tiled=True)  18.3 us
    all_gather x1, blocking collectives, body(): total_sq = jnp.sum(lax.all_gather(squares, 'ch'), axis=0)  15.8 us
    pallas_call x1, Pallas kernels, causal_conv(): pl.pallas_call(lambda *refs: conv_kernel(width, *refs), out_shape=jax.Sha...  7.93 us
  transfers between devices with their start and end apart: 1, of which 1 were waited for; matrix products, arithmetic and copies ran while one was open for 1% of the time, Pallas kernels for 0%

profile of v9, /device:TPU:1, one launch (start us, length us, event | category | flops | bytes accessed | tf_op | source)
XLA Modules:
  0.0 93.6 jit_solution(379528783392723608)
XLA Ops:
  0.0 0.7 fusion.7
  0.7 1.0 %fusion.2 = bf16[512,128]{0,1:T(8,128)(2,1)S(1)} fusion(bf16[128,512]{1,0:T(8,128)(2,1)} %param.9, bf16[128,512]{1,0:T(8,128)(2,1)} %param.8), kind=kLoop, calls=%fused_computation.9 | loop fusion | flops 327680 | bytes 393216 | tf_op jit(solution)/shard_map/transpose | solution.py:122
  1.8 0.1 copy.14
  1.9 0.1 pad.6.clone
  2.0 0.8 maximum_maximum_fusion
  2.8 0.0 copy-start.4
  2.8 19.2 %all-to-all-start = ((bf16[64,16,128]{2,1,0:T(8,128)(2,1)}), bf16[64,16,128]{2,1,0:T(8,128)(2,1)S(1)}, u32[]{:S(2)}, u32[]{:S(2)}) async-start(bf16[64,16,128]{2,1,0:T(8,128)(2,1)} %maximum_maximum_fusion), calls=%async_computation | async-start | bytes 524288 | tf_op jit(solution)/shard_map/all_to_all | solution.py:128
  22.1 0.0 copy-done.4
  22.2 0.8 select_reduce_fusion.refs_0_
  22.9 18.3 %all-to-all-done.refs_3_ = bf16[64,16,128]{2,1,0:T(8,128)(2,1)S(1)} async-done(((bf16[64,16,128]{2,1,0:T(8,128)(2,1)}), bf16[64,16,128]{2,1,0:T(8,128)(2,1)S(1)}, u32[]{:S(2)}, u32[]{:S(2)}) %all-to-all-start) | async-done | bytes 262176 | tf_op jit(solution)/shard_map/all_to_all | solution.py:128
  41.3 0.0 copy-start.3
  41.3 0.1 fusion.4
  41.5 0.7 subtract_reduce-precision_fusion
  42.1 0.0 copy-done.3
  42.1 7.9 %shard_map.73 = f32[64,8,128]{2,1,0:T(8,128)} custom-call(s32[64]{0:T(128)} %select_reduce_fusion.refs_0_, f32[16,768]{1,0:T(8,128)} %get-tuple-element.8.refs_1_, f32[16,768]{1,0:T(8,128)} %get-tuple-element.7.refs_2_, bf16[64,16,128]{2,1,0:T(8,128)(2,1)} %copy-done.3), custom_call_target="tpu_custom_call" | custom-call | flops 2147483648 | bytes 573440 | tf_op jit(solution)/shard_map/pallas_call | solution.py:90
  50.1 25.7 %all_to_all.10 = f32[64,8,128]{2,1,0:T(8,128)S(1)} all-to-all(f32[64,8,128]{2,1,0:T(8,128)} %shard_map.73), channel_id=1, replica_groups=mesh['ctx'=64,'ch'=8] {'ctx'}, dimensions={0} | all-to-all | bytes 524288 | tf_op jit(solution)/shard_map/all_to_all | solution.py:137
  75.8 0.0 copy-start
  75.8 0.0 copy-start.1
  75.8 0.0 copy-start.2
  75.8 0.0 copy-start.5
  75.8 0.1 copy.16
  75.9 0.8 copy-done
  76.7 0.1 copy-done.1
  76.8 0.1 copy-done.2
  76.8 0.0 copy-done.5
  76.8 0.0 copy-start.6
  76.8 0.2 multiply_reduce_fusion
  77.0 15.8 %all-gather.1 = f32[8,1,128]{2,1,0:T(1,128)S(1)} all-gather(f32[1,1,128]{2,1,0:T(1,128)S(1)} %bitcast.19), channel_id=2, replica_groups=mesh['ctx'=64,'ch'=8] {'ch'}, dimensions={0}, use_global_device_ids=true | all-gather | bytes 4608 | tf_op jit(solution)/shard_map/all_gather | solution.py:143
  92.9 0.0 copy-done.6
  92.9 0.8 multiply_convert_fusion
  (14 shorter events, 0.3 us)
Async XLA Ops:
  2.8 19.3 %copy-start.4 = (s32[2080,3]{0,1:T(4,128)S(1)}, s32[2080,3]{0,1:T(4,128)}, u32[]{:S(2)}) copy-start(s32[2080,3]{0,1:T(4,128)} %param.13) | copy-start | bytes 74884
  2.8 38.5 %all-to-all-start = ((bf16[64,16,128]{2,1,0:T(8,128)(2,1)}), bf16[64,16,128]{2,1,0:T(8,128)(2,1)S(1)}, u32[]{:S(2)}, u32[]{:S(2)}) async-start(bf16[64,16,128]{2,1,0:T(8,128)(2,1)} %maximum_maximum_fusion), calls=%async_computation | async-start | bytes 524288 | tf_op jit(solution)/shard_map/all_to_all | solution.py:128
  41.3 0.9 copy-start.3
  75.8 0.9 copy-start
  75.8 1.0 %copy-start.1 = (bf16[128,512]{1,0:T(8,128)(2,1)S(1)}, bf16[128,512]{1,0:T(8,128)(2,1)}, u32[]{:S(2)}) copy-start(bf16[128,512]{1,0:T(8,128)(2,1)} %param.8) | copy-start | bytes 393220
  75.8 1.0 %copy-start.2 = (bf16[128,512]{1,0:T(8,128)(2,1)S(1)}, bf16[128,512]{1,0:T(8,128)(2,1)}, u32[]{:S(2)}) copy-start(bf16[128,512]{1,0:T(8,128)(2,1)} %param.7) | copy-start | bytes 393220
  75.8 1.0 %copy-start.5 = (f32[512]{0:T(512)S(1)}, f32[512]{0:T(512)}, u32[]{:S(2)}) copy-start(f32[512]{0:T(512)} %param.11) | copy-start | bytes 6148
  76.8 16.0 %copy-start.6 = (f32[512]{0:T(512)S(1)}, f32[512]{0:T(512)}, u32[]{:S(2)}) copy-start(f32[512]{0:T(512)} %param.12) | copy-start | bytes 6148

commit v10 on v9

--- a/solution.py
+++ b/solution.py
@@ -23,12 +23,22 @@
     return lax.reduce_precision(values, exponent_bits=8, mantissa_bits=7)
 
 
-def conv_kernel(width, device_ref, window_ref, window_lo_ref, incoming_ref, out_ref, padded_ref):
+def conv_kernel(width, device_ref, incoming_ref, out_ref, padded_ref, window_ref, window_lo_ref):
+    part = out_ref.shape[2]
     rows = window_ref.shape[1] // 3
     pairs = window_ref.shape[0]
-    part = out_ref.shape[2]
     lanes = 2 * pairs * width
-    half = lanes // 2
+    pieces = rows // part
+    for pair in range(pairs):
+        for slot in range(3 * pieces):
+            source = (2 * pair - 1) * pieces + slot
+            for ref, line in ((window_ref, width), (window_lo_ref, width + 1)):
+                if source < 0:
+                    ref[pl.ds(pair, 1), pl.ds(slot * part, part)] = jnp.zeros((1, part), jnp.float32)
+                else:
+                    ref[pl.ds(pair, 1), pl.ds(slot * part, part)] = incoming_ref[
+                        source, pl.ds(line, 1), :
+                    ].astype(jnp.float32)
     padded_ref[pl.ds(0, lanes), :] = jnp.zeros((lanes, rows), jnp.float32)
     for block in range(incoming_ref.shape[0]):
         line = lanes + (block // (rows // part)) * width
@@ -81,24 +91,27 @@
         total = total[quarter:]
 
 
-def causal_conv(device_of, window, incoming, width):
-    window_hi = to_bf16_grid(window)
-    window_lo = to_bf16_grid(window - window_hi)
+def causal_conv(device_of, incoming, width):
     blocks, _, part = incoming.shape
-    rows = window.shape[1] // 3
-    lanes = blocks * part // rows * width
+    rows = 2 * part
+    pairs = blocks * part // (2 * rows)
+    lanes = 2 * pairs * width
     return pl.pallas_call(
         lambda *refs: conv_kernel(width, *refs),
         out_shape=jax.ShapeDtypeStruct((blocks, width, part), jnp.float32),
-        in_specs=[pl.BlockSpec(memory_space=pltpu.SMEM)] + [pl.BlockSpec(memory_space=pltpu.VMEM)] * 3,
+        in_specs=[pl.BlockSpec(memory_space=pltpu.SMEM), pl.BlockSpec(memory_space=pltpu.VMEM)],
         out_specs=pl.BlockSpec(memory_space=pltpu.VMEM),
-        scratch_shapes=[pltpu.VMEM((2 * lanes, rows), jnp.float32)],
+        scratch_shapes=[
+            pltpu.VMEM((2 * lanes, rows), jnp.float32),
+            pltpu.VMEM((pairs, 3 * rows), jnp.float32),
+            pltpu.VMEM((pairs, 3 * rows), jnp.float32),
+        ],
         cost_estimate=pl.CostEstimate(
-            flops=4 * rows * rows * lanes * 2 * window.shape[0],
-            bytes_accessed=window.size * 4 + incoming.size * 2 + rows * lanes * 4,
+            flops=4 * rows * rows * lanes * 2 * pairs,
+            bytes_accessed=incoming.size * 2 + rows * lanes * 4,
             transcendentals=0,
         ),
-    )(device_of, window_hi, window_lo, incoming)
+    )(device_of, incoming)
 
 
 def body(query, key, value, filter_taps, conv_bias, norm_gain, pair_list):
@@ -126,14 +139,7 @@
         axis=1,
     )
     incoming = lax.all_to_all(outgoing, "ctx", 0, 0, tiled=True)
-    taps_in = incoming[:, width : width + 2, :].astype(jnp.float32)
-    span = 2 * rows
-    wide = blocks // 2
-    my_taps = (taps_in[:, 0, :] + taps_in[:, 1, :]).reshape(wide, span)
-    shifted = jnp.concatenate([jnp.zeros((1, span), jnp.float32), my_taps], axis=0)
-    window = jnp.concatenate([shifted[0:-1:2], shifted[1::2], shifted[2::2]], axis=1)
-
-    conv = causal_conv(device_of, window, incoming, width)
+    conv = causal_conv(device_of, incoming, width)
     conv = lax.all_to_all(conv, "ctx", 0, 0, tiled=True)
     conv = conv.transpose(2, 0, 1).reshape(rows, channels)
 

time: 94 us -> 93.8 us (level)
  no operation moved by 1% of the time
where the time goes in v10:
time: 93.8 us; the launch traced here: 93.4 us
  blocking collectives  41.5 us (44%)
  starting transfers between devices  19.2 us (20%)
  waiting for transfers between devices  18.4 us (20%)
  Pallas kernels  7.92 us (8%)
  other arithmetic  4.29 us (5%)
  local copies, waits for them, and re-layouts  2 us (2%)
    all_to_all x1, blocking collectives, body(): conv = lax.all_to_all(conv, 'ctx', 0, 0, tiled=True)  25.7 us
    all_to_all x1, starting transfers between devices, body(): incoming = lax.all_to_all(outgoing, 'ctx', 0, 0, tiled=True)  19.2 us
    all_to_all x1, waiting for transfers between devices, body(): incoming = lax.all_to_all(outgoing, 'ctx', 0, 0, tiled=True)  18.4 us
    all_gather x1, blocking collectives, body(): total_sq = jnp.sum(lax.all_gather(squares, 'ch'), axis=0)  15.8 us
    pallas_call x1, Pallas kernels, causal_conv(): pl.pallas_call(lambda *refs: conv_kernel(width, *refs), out_shape=jax.Sha...  7.92 us
  transfers between devices with their start and end apart: 1, of which 1 were waited for; matrix products, arithmetic and copies ran while one was open for 1% of the time, Pallas kernels for 0%

profile of v10, /device:TPU:1, one launch (start us, length us, event | category | flops | bytes accessed | tf_op | source)
XLA Modules:
  0.0 93.4 jit_solution(8958389050894871741)
XLA Ops:
  0.0 0.7 fusion.5
  0.7 1.0 %fusion.2 = bf16[512,128]{0,1:T(8,128)(2,1)S(1)} fusion(bf16[128,512]{1,0:T(8,128)(2,1)} %param.9, bf16[128,512]{1,0:T(8,128)(2,1)} %param.8), kind=kLoop, calls=%fused_computation.9 | loop fusion | flops 327680 | bytes 393216 | tf_op jit(solution)/shard_map/transpose | solution.py:135
  1.8 0.1 copy.14
  1.9 0.1 pad.2.clone
  2.0 0.8 maximum_maximum_fusion
  2.8 0.0 copy-start.4
  2.8 19.2 %all-to-all-start = ((bf16[64,16,128]{2,1,0:T(8,128)(2,1)}), bf16[64,16,128]{2,1,0:T(8,128)(2,1)S(1)}, u32[]{:S(2)}, u32[]{:S(2)}) async-start(bf16[64,16,128]{2,1,0:T(8,128)(2,1)} %maximum_maximum_fusion), calls=%async_computation | async-start | bytes 524288 | tf_op jit(solution)/shard_map/all_to_all | solution.py:141
  22.1 0.0 copy-done.4
  22.2 0.7 select_reduce_fusion.refs_0_
  22.9 18.4 %all-to-all-done.refs_1_ = bf16[64,16,128]{2,1,0:T(8,128)(2,1)S(1)} async-done(((bf16[64,16,128]{2,1,0:T(8,128)(2,1)}), bf16[64,16,128]{2,1,0:T(8,128)(2,1)S(1)}, u32[]{:S(2)}, u32[]{:S(2)}) %all-to-all-start) | async-done | bytes 262176 | tf_op jit(solution)/shard_map/all_to_all | solution.py:141
  41.3 0.0 copy-start.3
  41.3 0.7 copy-done.3
  42.0 7.9 %shard_map.73 = f32[64,8,128]{2,1,0:T(8,128)} custom-call(s32[64]{0:T(128)} %select_reduce_fusion.refs_0_, bf16[64,16,128]{2,1,0:T(8,128)(2,1)} %copy-done.3), custom_call_target="tpu_custom_call" | custom-call | flops 2147483648 | bytes 524288 | tf_op jit(solution)/shard_map/pallas_call | solution.py:99
  49.9 25.7 %all_to_all.10 = f32[64,8,128]{2,1,0:T(8,128)S(1)} all-to-all(f32[64,8,128]{2,1,0:T(8,128)} %shard_map.73), channel_id=1, replica_groups=mesh['ctx'=64,'ch'=8] {'ctx'}, dimensions={0} | all-to-all | bytes 524288 | tf_op jit(solution)/shard_map/all_to_all | solution.py:143
  75.6 0.0 copy-start
  75.6 0.0 copy-start.1
  75.6 0.0 copy-start.2
  75.6 0.0 copy-start.5
  75.6 0.1 copy.16
  75.7 0.8 copy-done
  76.5 0.1 copy-done.1
  76.6 0.1 copy-done.2
  76.6 0.0 copy-done.5
  76.6 0.0 copy-start.6
  76.6 0.2 multiply_reduce_fusion
  76.8 15.8 %all-gather.1 = f32[8,1,128]{2,1,0:T(1,128)S(1)} all-gather(f32[1,1,128]{2,1,0:T(1,128)S(1)} %bitcast.19), channel_id=2, replica_groups=mesh['ctx'=64,'ch'=8] {'ch'}, dimensions={0}, use_global_device_ids=true | all-gather | bytes 4608 | tf_op jit(solution)/shard_map/all_gather | solution.py:149
  92.7 0.0 copy-done.6
  92.7 0.8 multiply_convert_fusion
  (8 shorter events, 0.2 us)
Async XLA Ops:
  2.8 19.3 %copy-start.4 = (s32[2080,3]{0,1:T(4,128)S(1)}, s32[2080,3]{0,1:T(4,128)}, u32[]{:S(2)}) copy-start(s32[2080,3]{0,1:T(4,128)} %param.13) | copy-start | bytes 74884
  2.8 38.5 %all-to-all-start = ((bf16[64,16,128]{2,1,0:T(8,128)(2,1)}), bf16[64,16,128]{2,1,0:T(8,128)(2,1)S(1)}, u32[]{:S(2)}, u32[]{:S(2)}) async-start(bf16[64,16,128]{2,1,0:T(8,128)(2,1)} %maximum_maximum_fusion), calls=%async_computation | async-start | bytes 524288 | tf_op jit(solution)/shard_map/all_to_all | solution.py:141
  41.3 0.7 copy-start.3
  75.6 0.9 copy-start
  75.6 1.0 %copy-start.1 = (bf16[128,512]{1,0:T(8,128)(2,1)S(1)}, bf16[128,512]{1,0:T(8,128)(2,1)}, u32[]{:S(2)}) copy-start(bf16[128,512]{1,0:T(8,128)(2,1)} %param.8) | copy-start | bytes 393220
  75.6 1.0 %copy-start.2 = (bf16[128,512]{1,0:T(8,128)(2,1)S(1)}, bf16[128,512]{1,0:T(8,128)(2,1)}, u32[]{:S(2)}) copy-start(bf16[128,512]{1,0:T(8,128)(2,1)} %param.7) | copy-start | bytes 393220
  75.6 1.0 %copy-start.5 = (f32[512]{0:T(512)S(1)}, f32[512]{0:T(512)}, u32[]{:S(2)}) copy-start(f32[512]{0:T(512)} %param.11) | copy-start | bytes 6148
  76.6 16.0 %copy-start.6 = (f32[512]{0:T(512)S(1)}, f32[512]{0:T(512)}, u32[]{:S(2)}) copy-start(f32[512]{0:T(512)} %param.12) | copy-start | bytes 6148

commit v11 on v10

--- a/solution.py
+++ b/solution.py
@@ -23,7 +23,7 @@
     return lax.reduce_precision(values, exponent_bits=8, mantissa_bits=7)
 
 
-def conv_kernel(width, device_ref, incoming_ref, out_ref, padded_ref, window_ref, window_lo_ref):
+def conv_kernel(width, device_ref, incoming_ref, out_ref, padded_ref, window_ref, window_lo_ref, even_ref, odd_ref):
     part = out_ref.shape[2]
     rows = window_ref.shape[1] // 3
     pairs = window_ref.shape[0]
@@ -47,9 +47,14 @@
             device_ref[block], pl.ds(0, width), :
         ].astype(jnp.float32)
 
-    def add_lag(total, block_hi, block_lo, lag, offset, count):
-        start = pl.multiple_of(lanes - lag * width + offset, width)
-        moved = padded_ref[pl.ds(start, count), :].astype(jnp.bfloat16)
+    padded_ref[pl.ds(2 * lanes, width), :] = jnp.zeros((width, rows), jnp.float32)
+    even_ref[...] = padded_ref[pl.ds(0, 2 * lanes), :].astype(jnp.bfloat16)
+    odd_ref[...] = padded_ref[pl.ds(width, 2 * lanes), :].astype(jnp.bfloat16)
+
+    def add_lag(total, block_hi, block_lo, pair, parity, offset, count):
+        source = odd_ref if parity else even_ref
+        start = pl.multiple_of(lanes - 2 * width * (pair + parity) + offset, 2 * width)
+        moved = source[pl.ds(start, count), :]
         total = total + jnp.dot(moved, block_hi, preferred_element_type=jnp.float32)
         return total + jnp.dot(moved, block_lo, preferred_element_type=jnp.float32)
 
@@ -61,12 +66,12 @@
         high = skew(window_ref, pair)
         low = skew(window_lo_ref, pair)
         first = (high[:, :rows].astype(jnp.bfloat16), low[:, :rows].astype(jnp.bfloat16))
-        total = add_lag(total, *first, 2 * pair, offset, count)
+        total = add_lag(total, *first, pair, 0, offset, count)
         second = (
             high[:, rows : 2 * rows].astype(jnp.bfloat16),
             low[:, rows : 2 * rows].astype(jnp.bfloat16),
         )
-        return add_lag(total, *second, 2 * pair + 1, offset, count)
+        return add_lag(total, *second, pair, 1, offset, count)
 
     def place(values, first):
         for row in range(values.shape[0] // width):
@@ -102,9 +107,11 @@
         in_specs=[pl.BlockSpec(memory_space=pltpu.SMEM), pl.BlockSpec(memory_space=pltpu.VMEM)],
         out_specs=pl.BlockSpec(memory_space=pltpu.VMEM),
         scratch_shapes=[
-            pltpu.VMEM((2 * lanes, rows), jnp.float32),
+            pltpu.VMEM((2 * lanes + width, rows), jnp.float32),
             pltpu.VMEM((pairs, 3 * rows), jnp.float32),
             pltpu.VMEM((pairs, 3 * rows), jnp.float32),
+            pltpu.VMEM((2 * lanes, rows), jnp.bfloat16),
+            pltpu.VMEM((2 * lanes, rows), jnp.bfloat16),
         ],
         cost_estimate=pl.CostEstimate(
             flops=4 * rows * rows * lanes * 2 * pairs,

time: 93.8 us -> 93.8 us (level)
  no operation moved by 1% of the time
where the time goes in v11:
time: 93.8 us; the launch traced here: 93.4 us
  blocking collectives  41.5 us (44%)
  starting transfers between devices  19.2 us (20%)
  waiting for transfers between devices  18.4 us (20%)
  Pallas kernels  7.94 us (8%)
  other arithmetic  4.29 us (5%)
  local copies, waits for them, and re-layouts  2 us (2%)
    all_to_all x1, blocking collectives, body(): conv = lax.all_to_all(conv, 'ctx', 0, 0, tiled=True)  25.7 us
    all_to_all x1, starting transfers between devices, body(): incoming = lax.all_to_all(outgoing, 'ctx', 0, 0, tiled=True)  19.2 us
    all_to_all x1, waiting for transfers between devices, body(): incoming = lax.all_to_all(outgoing, 'ctx', 0, 0, tiled=True)  18.4 us
    all_gather x1, blocking collectives, body(): total_sq = jnp.sum(lax.all_gather(squares, 'ch'), axis=0)  15.8 us
    pallas_call x1, Pallas kernels, causal_conv(): pl.pallas_call(lambda *refs: conv_kernel(width, *refs), out_shape=jax.Sha...  7.94 us
  transfers between devices with their start and end apart: 1, of which 1 were waited for; matrix products, arithmetic and copies ran while one was open for 1% of the time, Pallas kernels for 0%

profile of v11, /device:TPU:1, one launch (start us, length us, event | category | flops | bytes accessed | tf_op | source)
XLA Modules:
  0.0 93.4 jit_solution(17544186206675422209)
XLA Ops:
  0.0 0.7 fusion.5
  0.7 1.0 %fusion.2 = bf16[512,128]{0,1:T(8,128)(2,1)S(1)} fusion(bf16[128,512]{1,0:T(8,128)(2,1)} %param.9, bf16[128,512]{1,0:T(8,128)(2,1)} %param.8), kind=kLoop, calls=%fused_computation.9 | loop fusion | flops 327680 | bytes 393216 | tf_op jit(solution)/shard_map/transpose | solution.py:142
  1.8 0.1 copy.14
  1.9 0.1 pad.2.clone
  2.0 0.8 maximum_maximum_fusion
  2.8 0.0 copy-start.4
  2.8 19.2 %all-to-all-start = ((bf16[64,16,128]{2,1,0:T(8,128)(2,1)}), bf16[64,16,128]{2,1,0:T(8,128)(2,1)S(1)}, u32[]{:S(2)}, u32[]{:S(2)}) async-start(bf16[64,16,128]{2,1,0:T(8,128)(2,1)} %maximum_maximum_fusion), calls=%async_computation | async-start | bytes 524288 | tf_op jit(solution)/shard_map/all_to_all | solution.py:148
  22.1 0.0 copy-done.4
  22.2 0.7 select_reduce_fusion.refs_0_
  22.9 18.4 %all-to-all-done.refs_1_ = bf16[64,16,128]{2,1,0:T(8,128)(2,1)S(1)} async-done(((bf16[64,16,128]{2,1,0:T(8,128)(2,1)}), bf16[64,16,128]{2,1,0:T(8,128)(2,1)S(1)}, u32[]{:S(2)}, u32[]{:S(2)}) %all-to-all-start) | async-done | bytes 262176 | tf_op jit(solution)/shard_map/all_to_all | solution.py:148
  41.3 0.0 copy-start.3
  41.3 0.7 copy-done.3
  42.0 7.9 %shard_map.73 = f32[64,8,128]{2,1,0:T(8,128)} custom-call(s32[64]{0:T(128)} %select_reduce_fusion.refs_0_, bf16[64,16,128]{2,1,0:T(8,128)(2,1)} %copy-done.3), custom_call_target="tpu_custom_call" | custom-call | flops 2147483648 | bytes 524288 | tf_op jit(solution)/shard_map/pallas_call | solution.py:104
  49.9 25.7 %all_to_all.10 = f32[64,8,128]{2,1,0:T(8,128)S(1)} all-to-all(f32[64,8,128]{2,1,0:T(8,128)} %shard_map.73), channel_id=1, replica_groups=mesh['ctx'=64,'ch'=8] {'ctx'}, dimensions={0} | all-to-all | bytes 524288 | tf_op jit(solution)/shard_map/all_to_all | solution.py:150
  75.6 0.0 copy-start
  75.6 0.0 copy-start.1
  75.6 0.0 copy-start.2
  75.6 0.0 copy-start.5
  75.6 0.1 copy.16
  75.8 0.8 copy-done
  76.5 0.1 copy-done.1
  76.6 0.1 copy-done.2
  76.6 0.0 copy-done.5
  76.6 0.0 copy-start.6
  76.6 0.2 multiply_reduce_fusion
  76.8 15.8 %all-gather.1 = f32[8,1,128]{2,1,0:T(1,128)S(1)} all-gather(f32[1,1,128]{2,1,0:T(1,128)S(1)} %bitcast.19), channel_id=2, replica_groups=mesh['ctx'=64,'ch'=8] {'ch'}, dimensions={0}, use_global_device_ids=true | all-gather | bytes 4608 | tf_op jit(solution)/shard_map/all_gather | solution.py:156
  92.7 0.0 copy-done.6
  92.7 0.8 multiply_convert_fusion
  (8 shorter events, 0.2 us)
Async XLA Ops:
  2.8 19.3 %copy-start.4 = (s32[2080,3]{0,1:T(4,128)S(1)}, s32[2080,3]{0,1:T(4,128)}, u32[]{:S(2)}) copy-start(s32[2080,3]{0,1:T(4,128)} %param.13) | copy-start | bytes 74884
  2.8 38.5 %all-to-all-start = ((bf16[64,16,128]{2,1,0:T(8,128)(2,1)}), bf16[64,16,128]{2,1,0:T(8,128)(2,1)S(1)}, u32[]{:S(2)}, u32[]{:S(2)}) async-start(bf16[64,16,128]{2,1,0:T(8,128)(2,1)} %maximum_maximum_fusion), calls=%async_computation | async-start | bytes 524288 | tf_op jit(solution)/shard_map/all_to_all | solution.py:148
  41.3 0.7 copy-start.3
  75.6 0.9 copy-start
  75.6 1.0 %copy-start.1 = (bf16[128,512]{1,0:T(8,128)(2,1)S(1)}, bf16[128,512]{1,0:T(8,128)(2,1)}, u32[]{:S(2)}) copy-start(bf16[128,512]{1,0:T(8,128)(2,1)} %param.8) | copy-start | bytes 393220
  75.6 1.0 %copy-start.2 = (bf16[128,512]{1,0:T(8,128)(2,1)S(1)}, bf16[128,512]{1,0:T(8,128)(2,1)}, u32[]{:S(2)}) copy-start(bf16[128,512]{1,0:T(8,128)(2,1)} %param.7) | copy-start | bytes 393220
  75.6 1.0 %copy-start.5 = (f32[512]{0:T(512)S(1)}, f32[512]{0:T(512)}, u32[]{:S(2)}) copy-start(f32[512]{0:T(512)} %param.11) | copy-start | bytes 6148
  76.6 16.0 %copy-start.6 = (f32[512]{0:T(512)S(1)}, f32[512]{0:T(512)}, u32[]{:S(2)}) copy-start(f32[512]{0:T(512)} %param.12) | copy-start | bytes 6148

commit v12 on v10

--- a/solution.py
+++ b/solution.py
@@ -47,11 +47,9 @@
             device_ref[block], pl.ds(0, width), :
         ].astype(jnp.float32)
 
-    def add_lag(total, block_hi, block_lo, lag, offset, count):
+    def moved(lag, offset, count):
         start = pl.multiple_of(lanes - lag * width + offset, width)
-        moved = padded_ref[pl.ds(start, count), :].astype(jnp.bfloat16)
-        total = total + jnp.dot(moved, block_hi, preferred_element_type=jnp.float32)
-        return total + jnp.dot(moved, block_lo, preferred_element_type=jnp.float32)
+        return padded_ref[pl.ds(start, count), :].astype(jnp.bfloat16)
 
     def skew(ref, pair):
         window = jnp.broadcast_to(ref[pl.ds(pair, 1), :], (rows, 3 * rows))
@@ -60,13 +58,13 @@
     def add_pair(total, pair, offset, count):
         high = skew(window_ref, pair)
         low = skew(window_lo_ref, pair)
-        first = (high[:, :rows].astype(jnp.bfloat16), low[:, :rows].astype(jnp.bfloat16))
-        total = add_lag(total, *first, 2 * pair, offset, count)
-        second = (
-            high[:, rows : 2 * rows].astype(jnp.bfloat16),
-            low[:, rows : 2 * rows].astype(jnp.bfloat16),
-        )
-        return add_lag(total, *second, 2 * pair + 1, offset, count)
+        blocks = jnp.concatenate(
+            [high[:, :rows], low[:, :rows], high[:, rows : 2 * rows], low[:, rows : 2 * rows]], axis=0
+        ).astype(jnp.bfloat16)
+        first = moved(2 * pair, offset, count)
+        second = moved(2 * pair + 1, offset, count)
+        inputs = jnp.concatenate([first, first, second, second], axis=1)
+        return total + jnp.dot(inputs, blocks, preferred_element_type=jnp.float32)
 
     def place(values, first):
         for row in range(values.shape[0] // width):

time: 93.8 us -> 93.8 us (level)
  no operation moved by 1% of the time
where the time goes in v12:
time: 93.8 us; the launch traced here: 93.4 us
  blocking collectives  41.6 us (44%)
  starting transfers between devices  19.2 us (20%)
  waiting for transfers between devices  18.4 us (20%)
  Pallas kernels  7.9 us (8%)
  other arithmetic  4.29 us (5%)
  local copies, waits for them, and re-layouts  2 us (2%)
    all_to_all x1, blocking collectives, body(): conv = lax.all_to_all(conv, 'ctx', 0, 0, tiled=True)  25.7 us
    all_to_all x1, starting transfers between devices, body(): incoming = lax.all_to_all(outgoing, 'ctx', 0, 0, tiled=True)  19.2 us
    all_to_all x1, waiting for transfers between devices, body(): incoming = lax.all_to_all(outgoing, 'ctx', 0, 0, tiled=True)  18.4 us
    all_gather x1, blocking collectives, body(): total_sq = jnp.sum(lax.all_gather(squares, 'ch'), axis=0)  15.8 us
    pallas_call x1, Pallas kernels, causal_conv(): pl.pallas_call(lambda *refs: conv_kernel(width, *refs), out_shape=jax.Sha...  7.9 us
  transfers between devices with their start and end apart: 1, of which 1 were waited for; matrix products, arithmetic and copies ran while one was open for 1% of the time, Pallas kernels for 0%

profile of v12, /device:TPU:1, one launch (start us, length us, event | category | flops | bytes accessed | tf_op | source)
XLA Modules:
  0.0 93.4 jit_solution(15880036607348776609)
XLA Ops:
  0.0 0.7 fusion.5
  0.7 1.0 %fusion.2 = bf16[512,128]{0,1:T(8,128)(2,1)S(1)} fusion(bf16[128,512]{1,0:T(8,128)(2,1)} %param.9, bf16[128,512]{1,0:T(8,128)(2,1)} %param.8), kind=kLoop, calls=%fused_computation.9 | loop fusion | flops 327680 | bytes 393216 | tf_op jit(solution)/shard_map/transpose | solution.py:133
  1.8 0.1 copy.14
  1.9 0.1 pad.2.clone
  2.0 0.8 maximum_maximum_fusion
  2.8 0.0 copy-start.4
  2.8 19.2 %all-to-all-start = ((bf16[64,16,128]{2,1,0:T(8,128)(2,1)}), bf16[64,16,128]{2,1,0:T(8,128)(2,1)S(1)}, u32[]{:S(2)}, u32[]{:S(2)}) async-start(bf16[64,16,128]{2,1,0:T(8,128)(2,1)} %maximum_maximum_fusion), calls=%async_computation | async-start | bytes 524288 | tf_op jit(solution)/shard_map/all_to_all | solution.py:139
  22.1 0.0 copy-done.4
  22.2 0.7 select_reduce_fusion.refs_0_
  22.9 18.4 %all-to-all-done.refs_1_ = bf16[64,16,128]{2,1,0:T(8,128)(2,1)S(1)} async-done(((bf16[64,16,128]{2,1,0:T(8,128)(2,1)}), bf16[64,16,128]{2,1,0:T(8,128)(2,1)S(1)}, u32[]{:S(2)}, u32[]{:S(2)}) %all-to-all-start) | async-done | bytes 262176 | tf_op jit(solution)/shard_map/all_to_all | solution.py:139
  41.3 0.0 copy-start.3
  41.3 0.7 copy-done.3
  42.0 7.9 %shard_map.73 = f32[64,8,128]{2,1,0:T(8,128)} custom-call(s32[64]{0:T(128)} %select_reduce_fusion.refs_0_, bf16[64,16,128]{2,1,0:T(8,128)(2,1)} %copy-done.3), custom_call_target="tpu_custom_call" | custom-call | flops 2147483648 | bytes 524288 | tf_op jit(solution)/shard_map/pallas_call | solution.py:97
  49.9 25.7 %all_to_all.10 = f32[64,8,128]{2,1,0:T(8,128)S(1)} all-to-all(f32[64,8,128]{2,1,0:T(8,128)} %shard_map.73), channel_id=1, replica_groups=mesh['ctx'=64,'ch'=8] {'ctx'}, dimensions={0} | all-to-all | bytes 524288 | tf_op jit(solution)/shard_map/all_to_all | solution.py:141
  75.6 0.0 copy-start
  75.6 0.0 copy-start.1
  75.6 0.0 copy-start.2
  75.6 0.0 copy-start.5
  75.6 0.1 copy.16
  75.7 0.8 copy-done
  76.5 0.1 copy-done.1
  76.5 0.1 copy-done.2
  76.6 0.0 copy-done.5
  76.6 0.0 copy-start.6
  76.6 0.2 multiply_reduce_fusion
  76.8 15.8 %all-gather.1 = f32[8,1,128]{2,1,0:T(1,128)S(1)} all-gather(f32[1,1,128]{2,1,0:T(1,128)S(1)} %bitcast.19), channel_id=2, replica_groups=mesh['ctx'=64,'ch'=8] {'ch'}, dimensions={0}, use_global_device_ids=true | all-gather | bytes 4608 | tf_op jit(solution)/shard_map/all_gather | solution.py:147
  92.6 0.0 copy-done.6
  92.7 0.8 multiply_convert_fusion
  (8 shorter events, 0.2 us)
Async XLA Ops:
  2.8 19.3 %copy-start.4 = (s32[2080,3]{0,1:T(4,128)S(1)}, s32[2080,3]{0,1:T(4,128)}, u32[]{:S(2)}) copy-start(s32[2080,3]{0,1:T(4,128)} %param.13) | copy-start | bytes 74884
  2.8 38.5 %all-to-all-start = ((bf16[64,16,128]{2,1,0:T(8,128)(2,1)}), bf16[64,16,128]{2,1,0:T(8,128)(2,1)S(1)}, u32[]{:S(2)}, u32[]{:S(2)}) async-start(bf16[64,16,128]{2,1,0:T(8,128)(2,1)} %maximum_maximum_fusion), calls=%async_computation | async-start | bytes 524288 | tf_op jit(solution)/shard_map/all_to_all | solution.py:139
  41.3 0.7 copy-start.3
  75.6 0.9 copy-start
  75.6 1.0 %copy-start.1 = (bf16[128,512]{1,0:T(8,128)(2,1)S(1)}, bf16[128,512]{1,0:T(8,128)(2,1)}, u32[]{:S(2)}) copy-start(bf16[128,512]{1,0:T(8,128)(2,1)} %param.8) | copy-start | bytes 393220
  75.6 1.0 %copy-start.2 = (bf16[128,512]{1,0:T(8,128)(2,1)S(1)}, bf16[128,512]{1,0:T(8,128)(2,1)}, u32[]{:S(2)}) copy-start(bf16[128,512]{1,0:T(8,128)(2,1)} %param.7) | copy-start | bytes 393220
  75.6 1.0 %copy-start.5 = (f32[512]{0:T(512)S(1)}, f32[512]{0:T(512)}, u32[]{:S(2)}) copy-start(f32[512]{0:T(512)} %param.11) | copy-start | bytes 6148
  76.6 16.0 %copy-start.6 = (f32[512]{0:T(512)S(1)}, f32[512]{0:T(512)}, u32[]{:S(2)}) copy-start(f32[512]{0:T(512)} %param.12) | copy-start | bytes 6148

commit v13 on v10

--- a/solution.py
+++ b/solution.py
@@ -23,22 +23,12 @@
     return lax.reduce_precision(values, exponent_bits=8, mantissa_bits=7)
 
 
-def conv_kernel(width, device_ref, incoming_ref, out_ref, padded_ref, window_ref, window_lo_ref):
+def conv_kernel(width, device_ref, incoming_ref, out_ref, padded_ref):
     part = out_ref.shape[2]
-    rows = window_ref.shape[1] // 3
-    pairs = window_ref.shape[0]
+    rows = 2 * part
+    pairs = incoming_ref.shape[0] * part // (2 * rows)
     lanes = 2 * pairs * width
     pieces = rows // part
-    for pair in range(pairs):
-        for slot in range(3 * pieces):
-            source = (2 * pair - 1) * pieces + slot
-            for ref, line in ((window_ref, width), (window_lo_ref, width + 1)):
-                if source < 0:
-                    ref[pl.ds(pair, 1), pl.ds(slot * part, part)] = jnp.zeros((1, part), jnp.float32)
-                else:
-                    ref[pl.ds(pair, 1), pl.ds(slot * part, part)] = incoming_ref[
-                        source, pl.ds(line, 1), :
-                    ].astype(jnp.float32)
     padded_ref[pl.ds(0, lanes), :] = jnp.zeros((lanes, rows), jnp.float32)
     for block in range(incoming_ref.shape[0]):
         line = lanes + (block // (rows // part)) * width
@@ -53,13 +43,19 @@
         total = total + jnp.dot(moved, block_hi, preferred_element_type=jnp.float32)
         return total + jnp.dot(moved, block_lo, preferred_element_type=jnp.float32)
 
-    def skew(ref, pair):
-        window = jnp.broadcast_to(ref[pl.ds(pair, 1), :], (rows, 3 * rows))
+    def skew(line, pair):
+        columns = []
+        for slot in range(3 * pieces):
+            source = (2 * pair - 1) * pieces + slot
+            taps = incoming_ref[jnp.maximum(source, 0), pl.ds(line, 1), :].astype(jnp.float32)
+            taps = jnp.where(source >= 0, taps, 0.0)
+            columns.append(jnp.broadcast_to(taps, (rows, part)))
+        window = jnp.concatenate(columns, axis=1)
         return pltpu.roll(window, 2 * rows, 1, stride=1, stride_axis=0)
 
     def add_pair(total, pair, offset, count):
-        high = skew(window_ref, pair)
-        low = skew(window_lo_ref, pair)
+        high = skew(width, pair)
+        low = skew(width + 1, pair)
         first = (high[:, :rows].astype(jnp.bfloat16), low[:, :rows].astype(jnp.bfloat16))
         total = add_lag(total, *first, 2 * pair, offset, count)
         second = (
@@ -103,8 +99,6 @@
         out_specs=pl.BlockSpec(memory_space=pltpu.VMEM),
         scratch_shapes=[
             pltpu.VMEM((2 * lanes, rows), jnp.float32),
-            pltpu.VMEM((pairs, 3 * rows), jnp.float32),
-            pltpu.VMEM((pairs, 3 * rows), jnp.float32),
         ],
         cost_estimate=pl.CostEstimate(
             flops=4 * rows * rows * lanes * 2 * pairs,

time: 93.8 us -> 93.9 us (level)
  no operation moved by 1% of the time
where the time goes in v13:
time: 93.9 us; the launch traced here: 93.5 us
  blocking collectives  41.5 us (44%)
  starting transfers between devices  19.2 us (20%)
  waiting for transfers between devices  18.4 us (20%)
  Pallas kernels  8.03 us (9%)
  other arithmetic  4.29 us (5%)
  local copies, waits for them, and re-layouts  2 us (2%)
    all_to_all x1, blocking collectives, body(): conv = lax.all_to_all(conv, 'ctx', 0, 0, tiled=True)  25.7 us
    all_to_all x1, starting transfers between devices, body(): incoming = lax.all_to_all(outgoing, 'ctx', 0, 0, tiled=True)  19.2 us
    all_to_all x1, waiting for transfers between devices, body(): incoming = lax.all_to_all(outgoing, 'ctx', 0, 0, tiled=True)  18.4 us
    all_gather x1, blocking collectives, body(): total_sq = jnp.sum(lax.all_gather(squares, 'ch'), axis=0)  15.8 us
    pallas_call x1, Pallas kernels, causal_conv(): pl.pallas_call(lambda *refs: conv_kernel(width, *refs), out_shape=jax.Sha...  8.03 us
  transfers between devices with their start and end apart: 1, of which 1 were waited for; matrix products, arithmetic and copies ran while one was open for 1% of the time, Pallas kernels for 0%

profile of v13, /device:TPU:1, one launch (start us, length us, event | category | flops | bytes accessed | tf_op | source)
XLA Modules:
  0.0 93.5 jit_solution(12476706059421051937)
XLA Ops:
  0.0 0.7 fusion.5
  0.7 1.0 %fusion.2 = bf16[512,128]{0,1:T(8,128)(2,1)S(1)} fusion(bf16[128,512]{1,0:T(8,128)(2,1)} %param.9, bf16[128,512]{1,0:T(8,128)(2,1)} %param.8), kind=kLoop, calls=%fused_computation.9 | loop fusion | flops 327680 | bytes 393216 | tf_op jit(solution)/shard_map/transpose | solution.py:129
  1.8 0.1 copy.14
  1.9 0.1 pad.2.clone
  2.0 0.8 maximum_maximum_fusion
  2.8 0.0 copy-start.4
  2.8 19.2 %all-to-all-start = ((bf16[64,16,128]{2,1,0:T(8,128)(2,1)}), bf16[64,16,128]{2,1,0:T(8,128)(2,1)S(1)}, u32[]{:S(2)}, u32[]{:S(2)}) async-start(bf16[64,16,128]{2,1,0:T(8,128)(2,1)} %maximum_maximum_fusion), calls=%async_computation | async-start | bytes 524288 | tf_op jit(solution)/shard_map/all_to_all | solution.py:135
  22.1 0.0 copy-done.4
  22.2 0.7 select_reduce_fusion.refs_0_
  22.9 18.4 %all-to-all-done.refs_1_ = bf16[64,16,128]{2,1,0:T(8,128)(2,1)S(1)} async-done(((bf16[64,16,128]{2,1,0:T(8,128)(2,1)}), bf16[64,16,128]{2,1,0:T(8,128)(2,1)S(1)}, u32[]{:S(2)}, u32[]{:S(2)}) %all-to-all-start) | async-done | bytes 262176 | tf_op jit(solution)/shard_map/all_to_all | solution.py:135
  41.3 0.0 copy-start.3
  41.3 0.7 copy-done.3
  42.0 8.0 %shard_map.73 = f32[64,8,128]{2,1,0:T(8,128)} custom-call(s32[64]{0:T(128)} %select_reduce_fusion.refs_0_, bf16[64,16,128]{2,1,0:T(8,128)(2,1)} %copy-done.3), custom_call_target="tpu_custom_call" | custom-call | flops 2147483648 | bytes 524288 | tf_op jit(solution)/shard_map/pallas_call | solution.py:95
  50.0 25.7 %all_to_all.10 = f32[64,8,128]{2,1,0:T(8,128)S(1)} all-to-all(f32[64,8,128]{2,1,0:T(8,128)} %shard_map.73), channel_id=1, replica_groups=mesh['ctx'=64,'ch'=8] {'ctx'}, dimensions={0} | all-to-all | bytes 524288 | tf_op jit(solution)/shard_map/all_to_all | solution.py:137
  75.7 0.0 copy-start
  75.7 0.0 copy-start.1
  75.7 0.0 copy-start.2
  75.7 0.0 copy-start.5
  75.7 0.1 copy.16
  75.8 0.8 copy-done
  76.6 0.1 copy-done.1
  76.7 0.1 copy-done.2
  76.7 0.0 copy-done.5
  76.7 0.0 copy-start.6
  76.7 0.2 multiply_reduce_fusion
  76.9 15.8 %all-gather.1 = f32[8,1,128]{2,1,0:T(1,128)S(1)} all-gather(f32[1,1,128]{2,1,0:T(1,128)S(1)} %bitcast.19), channel_id=2, replica_groups=mesh['ctx'=64,'ch'=8] {'ch'}, dimensions={0}, use_global_device_ids=true | all-gather | bytes 4608 | tf_op jit(solution)/shard_map/all_gather | solution.py:143
  92.8 0.0 copy-done.6
  92.8 0.8 multiply_convert_fusion
  (8 shorter events, 0.2 us)
Async XLA Ops:
  2.8 19.3 %copy-start.4 = (s32[2080,3]{0,1:T(4,128)S(1)}, s32[2080,3]{0,1:T(4,128)}, u32[]{:S(2)}) copy-start(s32[2080,3]{0,1:T(4,128)} %param.13) | copy-start | bytes 74884
  2.8 38.5 %all-to-all-start = ((bf16[64,16,128]{2,1,0:T(8,128)(2,1)}), bf16[64,16,128]{2,1,0:T(8,128)(2,1)S(1)}, u32[]{:S(2)}, u32[]{:S(2)}) async-start(bf16[64,16,128]{2,1,0:T(8,128)(2,1)} %maximum_maximum_fusion), calls=%async_computation | async-start | bytes 524288 | tf_op jit(solution)/shard_map/all_to_all | solution.py:135
  41.3 0.7 copy-start.3
  75.7 0.9 copy-start
  75.7 1.0 %copy-start.1 = (bf16[128,512]{1,0:T(8,128)(2,1)S(1)}, bf16[128,512]{1,0:T(8,128)(2,1)}, u32[]{:S(2)}) copy-start(bf16[128,512]{1,0:T(8,128)(2,1)} %param.8) | copy-start | bytes 393220
  75.7 1.0 %copy-start.2 = (bf16[128,512]{1,0:T(8,128)(2,1)S(1)}, bf16[128,512]{1,0:T(8,128)(2,1)}, u32[]{:S(2)}) copy-start(bf16[128,512]{1,0:T(8,128)(2,1)} %param.7) | copy-start | bytes 393220
  75.7 1.0 %copy-start.5 = (f32[512]{0:T(512)S(1)}, f32[512]{0:T(512)}, u32[]{:S(2)}) copy-start(f32[512]{0:T(512)} %param.11) | copy-start | bytes 6148
  76.7 16.0 %copy-start.6 = (f32[512]{0:T(512)S(1)}, f32[512]{0:T(512)}, u32[]{:S(2)}) copy-start(f32[512]{0:T(512)} %param.12) | copy-start | bytes 6148

commit v14 on v10

--- a/solution.py
+++ b/solution.py
@@ -86,6 +86,7 @@
             (index + 1) * pairs // quarters,
             lambda pair, acc, first=first: add_pair(acc, pair, first, lanes - first),
             total,
+            unroll=True,
         )
         place(total[:quarter], first // width)
         total = total[quarter:]

time: 93.8 us -> 90 us (0.959)
  Pallas kernels: 7.92 us -> 4.13 us
    pallas_call x1, Pallas kernels: 7.92 us -> 4.13 us  [causal_conv(): pl.pallas_call(lambda *refs: conv_kernel(width, *refs), out_shape=jax.Sha...]
where the time goes in v14:
time: 90 us; the launch traced here: 89.6 us
  blocking collectives  41.5 us (46%)
  starting transfers between devices  19.2 us (21%)
  waiting for transfers between devices  18.4 us (20%)
  other arithmetic  4.29 us (5%)
  Pallas kernels  4.13 us (5%)
  local copies, waits for them, and re-layouts  2 us (2%)
    all_to_all x1, blocking collectives, body(): conv = lax.all_to_all(conv, 'ctx', 0, 0, tiled=True)  25.7 us
    all_to_all x1, starting transfers between devices, body(): incoming = lax.all_to_all(outgoing, 'ctx', 0, 0, tiled=True)  19.2 us
    all_to_all x1, waiting for transfers between devices, body(): incoming = lax.all_to_all(outgoing, 'ctx', 0, 0, tiled=True)  18.4 us
    all_gather x1, blocking collectives, body(): total_sq = jnp.sum(lax.all_gather(squares, 'ch'), axis=0)  15.8 us
    pallas_call x1, Pallas kernels, causal_conv(): pl.pallas_call(lambda *refs: conv_kernel(width, *refs), out_shape=jax.Sha...  4.13 us
  transfers between devices with their start and end apart: 1, of which 1 were waited for; matrix products, arithmetic and copies ran while one was open for 1% of the time, Pallas kernels for 0%

profile of v14, /device:TPU:1, one launch (start us, length us, event | category | flops | bytes accessed | tf_op | source)
XLA Modules:
  0.0 89.6 jit_solution(6401553076067516139)
XLA Ops:
  0.0 0.7 fusion.5
  0.7 1.0 %fusion.2 = bf16[512,128]{0,1:T(8,128)(2,1)S(1)} fusion(bf16[128,512]{1,0:T(8,128)(2,1)} %param.9, bf16[128,512]{1,0:T(8,128)(2,1)} %param.8), kind=kLoop, calls=%fused_computation.9 | loop fusion | flops 327680 | bytes 393216 | tf_op jit(solution)/shard_map/transpose | solution.py:136
  1.8 0.1 copy.14
  1.9 0.1 pad.2.clone
  2.0 0.8 maximum_maximum_fusion
  2.8 0.0 copy-start.4
  2.8 19.2 %all-to-all-start = ((bf16[64,16,128]{2,1,0:T(8,128)(2,1)}), bf16[64,16,128]{2,1,0:T(8,128)(2,1)S(1)}, u32[]{:S(2)}, u32[]{:S(2)}) async-start(bf16[64,16,128]{2,1,0:T(8,128)(2,1)} %maximum_maximum_fusion), calls=%async_computation | async-start | bytes 524288 | tf_op jit(solution)/shard_map/all_to_all | solution.py:142
  22.1 0.0 copy-done.4
  22.2 0.7 select_reduce_fusion.refs_0_
  22.9 18.4 %all-to-all-done.refs_1_ = bf16[64,16,128]{2,1,0:T(8,128)(2,1)S(1)} async-done(((bf16[64,16,128]{2,1,0:T(8,128)(2,1)}), bf16[64,16,128]{2,1,0:T(8,128)(2,1)S(1)}, u32[]{:S(2)}, u32[]{:S(2)}) %all-to-all-start) | async-done | bytes 262176 | tf_op jit(solution)/shard_map/all_to_all | solution.py:142
  41.3 0.0 copy-start.3
  41.3 0.7 copy-done.3
  42.0 4.1 %shard_map.73 = f32[64,8,128]{2,1,0:T(8,128)} custom-call(s32[64]{0:T(128)} %select_reduce_fusion.refs_0_, bf16[64,16,128]{2,1,0:T(8,128)(2,1)} %copy-done.3), custom_call_target="tpu_custom_call" | custom-call | flops 2147483648 | bytes 524288 | tf_op jit(solution)/shard_map/pallas_call | solution.py:100
  46.1 25.7 %all_to_all.10 = f32[64,8,128]{2,1,0:T(8,128)S(1)} all-to-all(f32[64,8,128]{2,1,0:T(8,128)} %shard_map.73), channel_id=1, replica_groups=mesh['ctx'=64,'ch'=8] {'ctx'}, dimensions={0} | all-to-all | bytes 524288 | tf_op jit(solution)/shard_map/all_to_all | solution.py:144
  71.8 0.0 copy-start
  71.8 0.0 copy-start.1
  71.8 0.0 copy-start.2
  71.8 0.0 copy-start.5
  71.8 0.1 copy.16
  72.0 0.8 copy-done
  72.7 0.1 copy-done.1
  72.8 0.1 copy-done.2
  72.8 0.0 copy-done.5
  72.8 0.0 copy-start.6
  72.8 0.2 multiply_reduce_fusion
  73.0 15.8 %all-gather.1 = f32[8,1,128]{2,1,0:T(1,128)S(1)} all-gather(f32[1,1,128]{2,1,0:T(1,128)S(1)} %bitcast.19), channel_id=2, replica_groups=mesh['ctx'=64,'ch'=8] {'ch'}, dimensions={0}, use_global_device_ids=true | all-gather | bytes 4608 | tf_op jit(solution)/shard_map/all_gather | solution.py:150
  88.9 0.0 copy-done.6
  88.9 0.8 multiply_convert_fusion
  (8 shorter events, 0.2 us)
Async XLA Ops:
  2.8 19.3 %copy-start.4 = (s32[2080,3]{0,1:T(4,128)S(1)}, s32[2080,3]{0,1:T(4,128)}, u32[]{:S(2)}) copy-start(s32[2080,3]{0,1:T(4,128)} %param.13) | copy-start | bytes 74884
  2.8 38.5 %all-to-all-start = ((bf16[64,16,128]{2,1,0:T(8,128)(2,1)}), bf16[64,16,128]{2,1,0:T(8,128)(2,1)S(1)}, u32[]{:S(2)}, u32[]{:S(2)}) async-start(bf16[64,16,128]{2,1,0:T(8,128)(2,1)} %maximum_maximum_fusion), calls=%async_computation | async-start | bytes 524288 | tf_op jit(solution)/shard_map/all_to_all | solution.py:142
  41.3 0.7 copy-start.3
  71.8 0.9 %copy-start = (bf16[128,512]{1,0:T(8,128)(2,1)S(1)}, bf16[128,512]{1,0:T(8,128)(2,1)}, u32[]{:S(2)}) copy-start(bf16[128,512]{1,0:T(8,128)(2,1)} %param.9) | copy-start | bytes 393220
  71.8 1.0 %copy-start.1 = (bf16[128,512]{1,0:T(8,128)(2,1)S(1)}, bf16[128,512]{1,0:T(8,128)(2,1)}, u32[]{:S(2)}) copy-start(bf16[128,512]{1,0:T(8,128)(2,1)} %param.8) | copy-start | bytes 393220
  71.8 1.0 %copy-start.2 = (bf16[128,512]{1,0:T(8,128)(2,1)S(1)}, bf16[128,512]{1,0:T(8,128)(2,1)}, u32[]{:S(2)}) copy-start(bf16[128,512]{1,0:T(8,128)(2,1)} %param.7) | copy-start | bytes 393220
  71.8 1.0 %copy-start.5 = (f32[512]{0:T(512)S(1)}, f32[512]{0:T(512)}, u32[]{:S(2)}) copy-start(f32[512]{0:T(512)} %param.11) | copy-start | bytes 6148
  72.8 16.0 %copy-start.6 = (f32[512]{0:T(512)S(1)}, f32[512]{0:T(512)}, u32[]{:S(2)}) copy-start(f32[512]{0:T(512)} %param.12) | copy-start | bytes 6148

commit v15 on v10

--- a/solution.py
+++ b/solution.py
@@ -76,19 +76,13 @@
                     row * width : (row + 1) * width, piece * part : (piece + 1) * part
                 ]
 
-    quarters = 4
-    quarter = lanes // quarters
+    step = 2 * width
     total = jnp.zeros((lanes, rows), jnp.float32)
-    for index in range(quarters):
-        first = index * quarter
-        total = lax.fori_loop(
-            index * pairs // quarters,
-            (index + 1) * pairs // quarters,
-            lambda pair, acc, first=first: add_pair(acc, pair, first, lanes - first),
-            total,
-        )
-        place(total[:quarter], first // width)
-        total = total[quarter:]
+    for pair in range(pairs):
+        first = pair * step
+        total = add_pair(total, pair, first, lanes - first)
+        place(total[:step], first // width)
+        total = total[step:]
 
 
 def causal_conv(device_of, incoming, width):

time: 93.8 us -> 89.9 us (0.958)
  Pallas kernels: 7.92 us -> 4.03 us
    pallas_call x1, Pallas kernels: 7.92 us -> 4.03 us  [causal_conv(): pl.pallas_call(lambda *refs: conv_kernel(width, *refs), out_shape=jax.Sha...]
where the time goes in v15:
time: 89.9 us; the launch traced here: 89.5 us
  blocking collectives  41.5 us (46%)
  starting transfers between devices  19.2 us (21%)
  waiting for transfers between devices  18.4 us (20%)
  other arithmetic  4.29 us (5%)
  Pallas kernels  4.03 us (4%)
  local copies, waits for them, and re-layouts  2 us (2%)
    all_to_all x1, blocking collectives, body(): conv = lax.all_to_all(conv, 'ctx', 0, 0, tiled=True)  25.7 us
    all_to_all x1, starting transfers between devices, body(): incoming = lax.all_to_all(outgoing, 'ctx', 0, 0, tiled=True)  19.2 us
    all_to_all x1, waiting for transfers between devices, body(): incoming = lax.all_to_all(outgoing, 'ctx', 0, 0, tiled=True)  18.4 us
    all_gather x1, blocking collectives, body(): total_sq = jnp.sum(lax.all_gather(squares, 'ch'), axis=0)  15.8 us
    pallas_call x1, Pallas kernels, causal_conv(): pl.pallas_call(lambda *refs: conv_kernel(width, *refs), out_shape=jax.Sha...  4.03 us
  transfers between devices with their start and end apart: 1, of which 1 were waited for; matrix products, arithmetic and copies ran while one was open for 1% of the time, Pallas kernels for 0%

profile of v15, /device:TPU:1, one launch (start us, length us, event | category | flops | bytes accessed | tf_op | source)
XLA Modules:
  0.0 89.5 jit_solution(10295133014744318711)
XLA Ops:
  0.0 0.7 fusion.5
  0.7 1.0 %fusion.2 = bf16[512,128]{0,1:T(8,128)(2,1)S(1)} fusion(bf16[128,512]{1,0:T(8,128)(2,1)} %param.9, bf16[128,512]{1,0:T(8,128)(2,1)} %param.8), kind=kLoop, calls=%fused_computation.9 | loop fusion | flops 327680 | bytes 393216 | tf_op jit(solution)/shard_map/transpose | solution.py:129
  1.8 0.1 copy.14
  1.9 0.1 pad.2.clone
  2.0 0.8 maximum_maximum_fusion
  2.8 0.0 copy-start.4
  2.8 19.2 %all-to-all-start = ((bf16[64,16,128]{2,1,0:T(8,128)(2,1)}), bf16[64,16,128]{2,1,0:T(8,128)(2,1)S(1)}, u32[]{:S(2)}, u32[]{:S(2)}) async-start(bf16[64,16,128]{2,1,0:T(8,128)(2,1)} %maximum_maximum_fusion), calls=%async_computation | async-start | bytes 524288 | tf_op jit(solution)/shard_map/all_to_all | solution.py:135
  22.1 0.0 copy-done.4
  22.2 0.7 select_reduce_fusion.refs_0_
  22.9 18.4 %all-to-all-done.refs_1_ = bf16[64,16,128]{2,1,0:T(8,128)(2,1)S(1)} async-done(((bf16[64,16,128]{2,1,0:T(8,128)(2,1)}), bf16[64,16,128]{2,1,0:T(8,128)(2,1)S(1)}, u32[]{:S(2)}, u32[]{:S(2)}) %all-to-all-start) | async-done | bytes 262176 | tf_op jit(solution)/shard_map/all_to_all | solution.py:135
  41.3 0.0 copy-start.3
  41.3 0.7 copy-done.3
  42.0 4.0 %shard_map.73 = f32[64,8,128]{2,1,0:T(8,128)} custom-call(s32[64]{0:T(128)} %select_reduce_fusion.refs_0_, bf16[64,16,128]{2,1,0:T(8,128)(2,1)} %copy-done.3), custom_call_target="tpu_custom_call" | custom-call | flops 2147483648 | bytes 524288 | tf_op jit(solution)/shard_map/pallas_call | solution.py:93
  46.0 25.7 %all_to_all.10 = f32[64,8,128]{2,1,0:T(8,128)S(1)} all-to-all(f32[64,8,128]{2,1,0:T(8,128)} %shard_map.73), channel_id=1, replica_groups=mesh['ctx'=64,'ch'=8] {'ctx'}, dimensions={0} | all-to-all | bytes 524288 | tf_op jit(solution)/shard_map/all_to_all | solution.py:137
  71.7 0.0 copy-start
  71.7 0.0 copy-start.1
  71.7 0.0 copy-start.2
  71.7 0.0 copy-start.5
  71.7 0.1 copy.16
  71.9 0.8 copy-done
  72.6 0.1 copy-done.1
  72.7 0.1 copy-done.2
  72.7 0.0 copy-done.5
  72.8 0.0 copy-start.6
  72.8 0.2 multiply_reduce_fusion
  72.9 15.8 %all-gather.1 = f32[8,1,128]{2,1,0:T(1,128)S(1)} all-gather(f32[1,1,128]{2,1,0:T(1,128)S(1)} %bitcast.19), channel_id=2, replica_groups=mesh['ctx'=64,'ch'=8] {'ch'}, dimensions={0}, use_global_device_ids=true | all-gather | bytes 4608 | tf_op jit(solution)/shard_map/all_gather | solution.py:143
  88.8 0.0 copy-done.6
  88.8 0.8 multiply_convert_fusion
  (8 shorter events, 0.2 us)
Async XLA Ops:
  2.8 19.3 %copy-start.4 = (s32[2080,3]{0,1:T(4,128)S(1)}, s32[2080,3]{0,1:T(4,128)}, u32[]{:S(2)}) copy-start(s32[2080,3]{0,1:T(4,128)} %param.13) | copy-start | bytes 74884
  2.8 38.5 %all-to-all-start = ((bf16[64,16,128]{2,1,0:T(8,128)(2,1)}), bf16[64,16,128]{2,1,0:T(8,128)(2,1)S(1)}, u32[]{:S(2)}, u32[]{:S(2)}) async-start(bf16[64,16,128]{2,1,0:T(8,128)(2,1)} %maximum_maximum_fusion), calls=%async_computation | async-start | bytes 524288 | tf_op jit(solution)/shard_map/all_to_all | solution.py:135
  41.3 0.7 copy-start.3
  71.7 0.9 %copy-start = (bf16[128,512]{1,0:T(8,128)(2,1)S(1)}, bf16[128,512]{1,0:T(8,128)(2,1)}, u32[]{:S(2)}) copy-start(bf16[128,512]{1,0:T(8,128)(2,1)} %param.9) | copy-start | bytes 393220
  71.7 1.0 %copy-start.1 = (bf16[128,512]{1,0:T(8,128)(2,1)S(1)}, bf16[128,512]{1,0:T(8,128)(2,1)}, u32[]{:S(2)}) copy-start(bf16[128,512]{1,0:T(8,128)(2,1)} %param.8) | copy-start | bytes 393220
  71.7 1.0 %copy-start.2 = (bf16[128,512]{1,0:T(8,128)(2,1)S(1)}, bf16[128,512]{1,0:T(8,128)(2,1)}, u32[]{:S(2)}) copy-start(bf16[128,512]{1,0:T(8,128)(2,1)} %param.7) | copy-start | bytes 393220
  71.7 1.0 %copy-start.5 = (f32[512]{0:T(512)S(1)}, f32[512]{0:T(512)}, u32[]{:S(2)}) copy-start(f32[512]{0:T(512)} %param.11) | copy-start | bytes 6148
  72.8 16.0 %copy-start.6 = (f32[512]{0:T(512)S(1)}, f32[512]{0:T(512)}, u32[]{:S(2)}) copy-start(f32[512]{0:T(512)} %param.12) | copy-start | bytes 6148

commit v16 on v12

--- a/solution.py
+++ b/solution.py
@@ -74,19 +74,13 @@
                     row * width : (row + 1) * width, piece * part : (piece + 1) * part
                 ]
 
-    quarters = 4
-    quarter = lanes // quarters
+    step = 2 * width
     total = jnp.zeros((lanes, rows), jnp.float32)
-    for index in range(quarters):
-        first = index * quarter
-        total = lax.fori_loop(
-            index * pairs // quarters,
-            (index + 1) * pairs // quarters,
-            lambda pair, acc, first=first: add_pair(acc, pair, first, lanes - first),
-            total,
-        )
-        place(total[:quarter], first // width)
-        total = total[quarter:]
+    for pair in range(pairs):
+        first = pair * step
+        total = add_pair(total, pair, first, lanes - first)
+        place(total[:step], first // width)
+        total = total[step:]
 
 
 def causal_conv(device_of, incoming, width):

time: 93.8 us -> 89.9 us (0.958)
  Pallas kernels: 7.9 us -> 4.01 us
    pallas_call x1, Pallas kernels: 7.9 us -> 4.01 us  [causal_conv(): pl.pallas_call(lambda *refs: conv_kernel(width, *refs), out_shape=jax.Sha...]
where the time goes in v16:
time: 89.9 us; the launch traced here: 89.5 us
  blocking collectives  41.5 us (46%)
  starting transfers between devices  19.2 us (21%)
  waiting for transfers between devices  18.4 us (20%)
  other arithmetic  4.29 us (5%)
  Pallas kernels  4.01 us (4%)
  local copies, waits for them, and re-layouts  2 us (2%)
    all_to_all x1, blocking collectives, body(): conv = lax.all_to_all(conv, 'ctx', 0, 0, tiled=True)  25.7 us
    all_to_all x1, starting transfers between devices, body(): incoming = lax.all_to_all(outgoing, 'ctx', 0, 0, tiled=True)  19.2 us
    all_to_all x1, waiting for transfers between devices, body(): incoming = lax.all_to_all(outgoing, 'ctx', 0, 0, tiled=True)  18.4 us
    all_gather x1, blocking collectives, body(): total_sq = jnp.sum(lax.all_gather(squares, 'ch'), axis=0)  15.8 us
    pallas_call x1, Pallas kernels, causal_conv(): pl.pallas_call(lambda *refs: conv_kernel(width, *refs), out_shape=jax.Sha...  4.01 us
  transfers between devices with their start and end apart: 1, of which 1 were waited for; matrix products, arithmetic and copies ran while one was open for 1% of the time, Pallas kernels for 0%

profile of v16, /device:TPU:1, one launch (start us, length us, event | category | flops | bytes accessed | tf_op | source)
XLA Modules:
  0.0 89.5 jit_solution(14331549769472900749)
XLA Ops:
  0.0 0.7 fusion.5
  0.7 1.0 %fusion.2 = bf16[512,128]{0,1:T(8,128)(2,1)S(1)} fusion(bf16[128,512]{1,0:T(8,128)(2,1)} %param.9, bf16[128,512]{1,0:T(8,128)(2,1)} %param.8), kind=kLoop, calls=%fused_computation.9 | loop fusion | flops 327680 | bytes 393216 | tf_op jit(solution)/shard_map/transpose | solution.py:127
  1.8 0.1 copy.14
  1.9 0.1 pad.2.clone
  2.0 0.8 maximum_maximum_fusion
  2.8 0.0 copy-start.4
  2.8 19.2 %all-to-all-start = ((bf16[64,16,128]{2,1,0:T(8,128)(2,1)}), bf16[64,16,128]{2,1,0:T(8,128)(2,1)S(1)}, u32[]{:S(2)}, u32[]{:S(2)}) async-start(bf16[64,16,128]{2,1,0:T(8,128)(2,1)} %maximum_maximum_fusion), calls=%async_computation | async-start | bytes 524288 | tf_op jit(solution)/shard_map/all_to_all | solution.py:133
  22.1 0.0 copy-done.4
  22.2 0.7 select_reduce_fusion.refs_0_
  22.9 18.4 %all-to-all-done.refs_1_ = bf16[64,16,128]{2,1,0:T(8,128)(2,1)S(1)} async-done(((bf16[64,16,128]{2,1,0:T(8,128)(2,1)}), bf16[64,16,128]{2,1,0:T(8,128)(2,1)S(1)}, u32[]{:S(2)}, u32[]{:S(2)}) %all-to-all-start) | async-done | bytes 262176 | tf_op jit(solution)/shard_map/all_to_all | solution.py:133
  41.3 0.0 copy-start.3
  41.3 0.7 copy-done.3
  42.0 4.0 %shard_map.73 = f32[64,8,128]{2,1,0:T(8,128)} custom-call(s32[64]{0:T(128)} %select_reduce_fusion.refs_0_, bf16[64,16,128]{2,1,0:T(8,128)(2,1)} %copy-done.3), custom_call_target="tpu_custom_call" | custom-call | flops 2147483648 | bytes 524288 | tf_op jit(solution)/shard_map/pallas_call | solution.py:91
  46.0 25.7 %all_to_all.10 = f32[64,8,128]{2,1,0:T(8,128)S(1)} all-to-all(f32[64,8,128]{2,1,0:T(8,128)} %shard_map.73), channel_id=1, replica_groups=mesh['ctx'=64,'ch'=8] {'ctx'}, dimensions={0} | all-to-all | bytes 524288 | tf_op jit(solution)/shard_map/all_to_all | solution.py:135
  71.7 0.0 copy-start
  71.7 0.0 copy-start.1
  71.7 0.0 copy-start.2
  71.7 0.0 copy-start.5
  71.7 0.1 copy.16
  71.8 0.8 copy-done
  72.6 0.1 copy-done.1
  72.7 0.1 copy-done.2
  72.7 0.0 copy-done.5
  72.7 0.0 copy-start.6
  72.7 0.2 multiply_reduce_fusion
  72.9 15.8 %all-gather.1 = f32[8,1,128]{2,1,0:T(1,128)S(1)} all-gather(f32[1,1,128]{2,1,0:T(1,128)S(1)} %bitcast.19), channel_id=2, replica_groups=mesh['ctx'=64,'ch'=8] {'ch'}, dimensions={0}, use_global_device_ids=true | all-gather | bytes 4608 | tf_op jit(solution)/shard_map/all_gather | solution.py:141
  88.8 0.0 copy-done.6
  88.8 0.8 multiply_convert_fusion
  (8 shorter events, 0.2 us)
Async XLA Ops:
  2.8 19.3 %copy-start.4 = (s32[2080,3]{0,1:T(4,128)S(1)}, s32[2080,3]{0,1:T(4,128)}, u32[]{:S(2)}) copy-start(s32[2080,3]{0,1:T(4,128)} %param.13) | copy-start | bytes 74884
  2.8 38.5 %all-to-all-start = ((bf16[64,16,128]{2,1,0:T(8,128)(2,1)}), bf16[64,16,128]{2,1,0:T(8,128)(2,1)S(1)}, u32[]{:S(2)}, u32[]{:S(2)}) async-start(bf16[64,16,128]{2,1,0:T(8,128)(2,1)} %maximum_maximum_fusion), calls=%async_computation | async-start | bytes 524288 | tf_op jit(solution)/shard_map/all_to_all | solution.py:133
  41.3 0.7 copy-start.3
  71.7 0.9 %copy-start = (bf16[128,512]{1,0:T(8,128)(2,1)S(1)}, bf16[128,512]{1,0:T(8,128)(2,1)}, u32[]{:S(2)}) copy-start(bf16[128,512]{1,0:T(8,128)(2,1)} %param.9) | copy-start | bytes 393220
  71.7 1.0 %copy-start.1 = (bf16[128,512]{1,0:T(8,128)(2,1)S(1)}, bf16[128,512]{1,0:T(8,128)(2,1)}, u32[]{:S(2)}) copy-start(bf16[128,512]{1,0:T(8,128)(2,1)} %param.8) | copy-start | bytes 393220
  71.7 1.0 %copy-start.2 = (bf16[128,512]{1,0:T(8,128)(2,1)S(1)}, bf16[128,512]{1,0:T(8,128)(2,1)}, u32[]{:S(2)}) copy-start(bf16[128,512]{1,0:T(8,128)(2,1)} %param.7) | copy-start | bytes 393220
  71.7 1.0 %copy-start.5 = (f32[512]{0:T(512)S(1)}, f32[512]{0:T(512)}, u32[]{:S(2)}) copy-start(f32[512]{0:T(512)} %param.11) | copy-start | bytes 6148
  72.7 16.0 %copy-start.6 = (f32[512]{0:T(512)S(1)}, f32[512]{0:T(512)}, u32[]{:S(2)}) copy-start(f32[512]{0:T(512)} %param.12) | copy-start | bytes 6148
